TPU v7x, 256 devices: a whole 4x4x8 slice. The times are simulated.
256 devices in a mesh: tm: 64 (over x, z_hi, y), tile: 4 (over z_lo, core).
Axes of the slice: x: 4, y: 4, z: 8 (z_hi: 4, z_lo: 2; z = z_hi * 2 + z_lo), core: 2. Of those that a mesh axis runs over, the one named last changes fastest.
Arguments:
- diag_blocks: float32 [128, 1024, 1024], P('tm', None, 'tile'), as said below
- upper_blocks: float32 [128, 1024, 1024], P('tm', None, 'tile')
- arrow_blocks: float32 [128, 64, 1024], P('tm')
- tip_block: float32 [64, 64], replicated, as said below
Outputs:
- red_diag: float32 [64, 1024, 1024], P(None, 'tm', 'tile')
- red_upper: float32 [64, 1024, 1024], P(None, 'tm', 'tile')
- red_arrow: float32 [64, 64, 1024], P('tm', None, 'tile')
- red_tip: float32 [64, 64], replicated
Inputs may be any that keep to these rules, and one draw needn't show every extreme that they name: `diag_blocks`: every diagonal block is symmetric, and Q is symmetric positive definite. `tip_block`: Symmetric.
All inputs are finite; a program needn't handle non-finite values.
Results may differ from a plain program's by a relative error of at most 0.00016.
Values sent between devices are 32-bit elements; how exact they have to be, the bound alone decides.
No kernel may reach another device: no remote copies, remote signals or barrier semaphores. Data moves between devices by JAX's collectives and lax.ppermute only.
A program may use at most 128 MiB of HBM per device.

v0:
```python
import jax
import jax.numpy as jnp
from jax import lax
from jax.sharding import PartitionSpec as P

precise = lax.Precision.HIGHEST


def shifted(value, axis, by):
    count = lax.axis_size(axis)
    pairs = [(i, i + by) for i in range(count) if 0 <= i + by < count]
    return lax.ppermute(value, axis, pairs)


def lower_solve(factor, rhs):
    return lax.linalg.triangular_solve(factor, rhs, left_side=True, lower=True)


def product(left, right):
    return jnp.dot(left.T, right, precision=precise)


def body(diag_blocks, upper_blocks, arrow_blocks, tip_block):
    strip_width = diag_blocks.shape[2]
    offset = lax.axis_index("tile") * strip_width
    upper_after = shifted(upper_blocks[0], "tm", -1)
    first_full = lax.all_gather(upper_blocks[1], "tile", axis=1, tiled=True)
    fill_strip = lax.dynamic_slice_in_dim(first_full, offset, strip_width, 0).T
    top_diag = diag_blocks[0]
    top_arrow = arrow_blocks[0].T
    tip_part = jnp.zeros(tip_block.shape, jnp.float32)
    pivot_strip = diag_blocks[1]
    branch_cols = arrow_blocks[1].T
    whole_pivot = lax.all_gather(pivot_strip, "tile", axis=1, tiled=True)
    factor = jnp.linalg.cholesky(whole_pivot)
    fill_solved = lower_solve(factor, fill_strip)
    link_strip = lower_solve(factor, upper_after)
    branch_solved = lower_solve(factor, branch_cols)
    link_all = lax.all_gather(link_strip, "tile", axis=1, tiled=True)
    fill_all = lax.all_gather(fill_solved, "tile", axis=1, tiled=True)
    top_diag = top_diag - product(fill_all, fill_solved)
    top_arrow = top_arrow - product(fill_all, branch_solved)
    tip_part = tip_part - product(branch_solved, branch_solved)
    next_diag = -product(link_all, link_strip)
    next_upper = -product(fill_all, link_strip)
    next_arrow = -product(branch_solved, link_strip)
    tip_total = lax.psum(tip_part, "tm")
    red_tip = tip_block + tip_total
    own_arrow = lax.dynamic_slice_in_dim(top_arrow, offset, strip_width, 0).T
    came_diag, came_upper, came_arrow = shifted((next_diag, next_upper, next_arrow), "tm", 1)
    whole_diag = top_diag + came_diag
    red_diag, red_upper = (
        lax.all_to_all(whole_diag[None], "tm", split_axis=1, concat_axis=0, tiled=True),
        lax.all_to_all(came_upper[None], "tm", split_axis=1, concat_axis=0, tiled=True),
    )
    red_arrow = (own_arrow + came_arrow)[None]
    return (red_diag, red_upper, red_arrow, red_tip)


def solution(mesh):
    return jax.shard_map(
        body,
        mesh=mesh,
        in_specs=(P("tm", None, "tile"), P("tm", None, "tile"), P("tm", None, None), P()),
        out_specs=(P(None, "tm", "tile"), P(None, "tm", "tile"), P("tm", None, "tile"), P()),
        check_vma=False,
    )
```

profile of v0, /device:TPU:32, one launch (start us, length us, event | category | flops | bytes accessed | tf_op | source)
XLA Modules:
  0.0 1108.6 jit_solution(9350084477107216875)
XLA Ops:
  13.0 66.3 %all-gather.11.cloned.1.call-done = f32[1,1024,1024]{1,2,0:T(8,128)} async-done(((f32[1,1024,256]{1,2,0:T(8,128)}), f32[1,1024,1024]{1,2,0:T(8,128)}) %all-gather.11.cloned.1.call-update) | async-done | bytes 4194320 | tf_op jit(solution)/shard_map/all_gather | solution.py:34
  79.3 5.4 copy.11
  84.7 4.4 fusion
  91.1 11.7 %cholesky.223 = f32[128,128]{1,0:T(8,128)S(1)} custom-call(f32[128,128]{1,0:T(8,128)S(1)} %cholesky.580), custom_call_target="Cholesky" | custom-call | tf_op jit(solution)/shard_map/jit(cholesky)/cholesky | solution.py:35
  102.8 2.5 cholesky.255
  105.3 9.8 custom-call.65
  115.1 2.3 constant_dynamic-update-slice_fusion.79
  119.0 12.0 %cholesky.244 = f32[128,128]{1,0:T(8,128)S(1)} custom-call(f32[128,128]{1,0:T(8,128)S(1)} %cholesky.584), custom_call_target="Cholesky" | custom-call | tf_op jit(solution)/shard_map/jit(cholesky)/cholesky | solution.py:35
  131.7 9.8 custom-call.66
  144.9 11.7 %cholesky.468 = f32[128,128]{1,0:T(8,128)S(1)} custom-call(f32[128,128]{1,0:T(8,128)S(1)} %cholesky.589), custom_call_target="Cholesky" | custom-call | tf_op jit(solution)/shard_map/jit(cholesky)/cholesky | solution.py:35
  157.2 9.8 custom-call.67
  168.2 2.3 convolution_subtract_fusion.3
  170.6 11.9 %cholesky.487 = f32[128,128]{1,0:T(8,128)S(1)} custom-call(f32[128,128]{1,0:T(8,128)S(1)} %cholesky.594), custom_call_target="Cholesky" | custom-call | tf_op jit(solution)/shard_map/jit(cholesky)/cholesky | solution.py:35
  183.1 9.8 custom-call.68
  194.0 2.3 convolution_subtract_fusion.4
  196.4 11.7 %cholesky.506 = f32[128,128]{1,0:T(8,128)S(1)} custom-call(f32[128,128]{1,0:T(8,128)S(1)} %cholesky.599), custom_call_target="Cholesky" | custom-call | tf_op jit(solution)/shard_map/jit(cholesky)/cholesky | solution.py:35
  208.7 10.2 custom-call.69
  222.2 11.7 %cholesky.526 = f32[128,128]{1,0:T(8,128)S(1)} custom-call(f32[128,128]{1,0:T(8,128)S(1)} %cholesky.604), custom_call_target="Cholesky" | custom-call | tf_op jit(solution)/shard_map/jit(cholesky)/cholesky | solution.py:35
  234.6 9.8 custom-call.70
  247.4 11.7 %cholesky.546 = f32[128,128]{1,0:T(8,128)S(1)} custom-call(f32[128,128]{1,0:T(8,128)S(1)} %cholesky.609), custom_call_target="Cholesky" | custom-call | tf_op jit(solution)/shard_map/jit(cholesky)/cholesky | solution.py:35
  259.7 9.8 custom-call.71
  272.2 11.7 %cholesky.564 = f32[128,128]{1,0:T(8,128)S(1)} custom-call(f32[128,128]{1,0:T(8,128)S(1)} %convolution_subtract_fusion.14), custom_call_target="Cholesky" | custom-call | tf_op jit(solution)/shard_map/jit(cholesky)/cholesky | solution.py:35
  294.3 4.8 select_select_fusion
  299.1 24.1 %while.5 = (s32[]{:T(128)}, f32[1024,1024]{1,0:T(8,128)}, s32[8,2]{0,1:T(2,128)S(1)}, f32[8,128,128]{2,1,0:T(8,128)S(1)}, s32[]{:T(128)}) while((s32[]{:T(128)}, f32[1024,1024]{1,0:T(8,128)}, s32[8,2]{0,1:T(2,128)S(1)}, f32[8,128,128]{2,1,0:T(8,128)S(1)}, s32[]{:T(128)}) %tuple.115), condition=%wide.while_cond, body=%wide.while_body.sunk | while | flops 2 | bytes 131189 | solution.py:16
  299.8 2.3 bitcast_dynamic-update-slice_fusion.2
  302.8 2.3 bitcast_dynamic-update-slice_fusion.2
  305.8 2.3 bitcast_dynamic-update-slice_fusion.2
  308.8 2.3 bitcast_dynamic-update-slice_fusion.2
  311.9 2.3 bitcast_dynamic-update-slice_fusion.2
  314.9 2.3 bitcast_dynamic-update-slice_fusion.2
  317.9 2.3 bitcast_dynamic-update-slice_fusion.2
  323.2 78.6 %custom-call.74 = f32[8,128,128]{1,2,0:T(8,128)S(1)} custom-call(f32[8,128,128]{2,1,0:T(8,128)S(1)} %get-tuple-element.27), custom_call_target="InvertDiagBlocksLowerTriangular" | custom-call | tf_op jit(solution)/shard_map/triangular_solve/custom-call.7 | solution.py:16
  434.9 2.4 convolution_subtract_fusion.10
  437.6 2.7 convolution_subtract_fusion.13
  441.7 46.0 %all-gather.9.cloned.1.call-done = f32[1024,1024]{1,0:T(8,128)} async-done(((f32[1024,256]{1,0:T(8,128)}), f32[1024,1024]{1,0:T(8,128)}) %all-gather.9.cloned.1.call-update) | async-done | bytes 4194320 | tf_op jit(solution)/shard_map/all_gather | solution.py:39
  487.7 10.0 convolution_negate_fusion.1
  497.7 4.6 collective-permute-start.1
  505.3 33.5 %all-gather.7.cloned.1.call-done = f32[1024,1024]{1,0:T(8,128)} async-done(((f32[1024,256]{1,0:T(8,128)}), f32[1024,1024]{1,0:T(8,128)}) %all-gather.7.cloned.1.call-update) | async-done | bytes 4194320 | tf_op jit(solution)/shard_map/all_gather | solution.py:40
  538.8 9.5 fusion.2
  550.4 55.6 %all-to-all-start = ((f32[1,1024,256]{2,0,1:T(1,128)}), f32[1,1024,256]{2,0,1:T(1,128)S(1)}, u32[]{:S(2)}, u32[]{:S(2)}) async-start(f32[1,1024,256]{2,0,1:T(1,128)} %copy.12), calls=%async_computation | async-start | bytes 2097152 | tf_op jit(solution)/shard_map/all_to_all | solution.py:53
  608.8 8.5 convolution_negate_fusion
  617.4 3.7 collective-permute-start.2
  626.9 22.7 %collective-permute-done.2 = f32[1024,256]{1,0:T(8,128)S(1)} collective-permute-done((f32[1024,256]{1,0:T(8,128)S(1)}, f32[1024,256]{1,0:T(8,128)S(1)}, u32[]{:S(2)}, u32[]{:S(2)}) %collective-permute-start.2) | collective-permute-done | bytes 1048608 | tf_op jit(solution)/shard_map/ppermute | solution.py:12
  651.6 6.2 all-to-all-done
  657.8 48.6 %all-to-all-start.1 = ((f32[1,1024,256]{2,0,1:T(1,128)}), f32[1,1024,256]{2,0,1:T(1,128)}, u32[]{:S(2)}, u32[]{:S(2)}) async-start(f32[1,1024,256]{2,0,1:T(1,128)} %copy.13), calls=%async_computation.1 | async-start | bytes 2097152 | tf_op jit(solution)/shard_map/all_to_all | solution.py:54
  712.1 3.4 collective-permute-start.3
  715.9 376.3 %psum.7 = f32[64,64]{1,0:T(8,128)S(1)} all-reduce(f32[64,64]{1,0:T(8,128)S(1)} %convolution_subtract_fusion.19), channel_id=1, replica_groups=mesh['tm'=64,'tile'=4] {'tm'}, use_global_device_ids=true, to_apply=%region_16.18 | all-reduce | flops 4096 | bytes 32768 | tf_op jit(solution)/shard_map/psum | solution.py:47
  1092.7 4.9 fusion.141
  (139 shorter events, 101.5 us)
Async XLA Ops:
  7.2 3.0 copy-start.5
  7.2 72.1 %all-gather.11.cloned.1.call-start = ((), (), s32[]{:S(2)}) async-start(), calls=%async_computation.4 | async-start | bytes 5242880 | tf_op jit(solution)/shard_map/all_gather | solution.py:34
  10.1 412.7 %all-gather.13.cloned.1.call-start = ((), (), s32[]{:S(2)}) async-start(), calls=%async_computation.5 | async-start | bytes 5242880 | tf_op jit(solution)/shard_map/all_gather | solution.py:27
  11.6 390.2 %collective-permute-start = (f32[1024,256]{1,0:T(8,128)}, f32[1024,256]{1,0:T(8,128)}, u32[]{:S(2)}, u32[]{:S(2)}) collective-permute-start(f32[1024,256]{1,0:T(8,128)} %get-tuple-element.40), channel_id=1, source_target_pairs={{4,0},{8,4},{12,8},{16,12},{20,16},{24,20},{28,24},{32,28},{36,32}... | collective-permute-start | bytes 3145736 | tf_op jit(solution)/shard_map/ppermute | solution.py:12
  12.9 474.8 %all-gather.9.cloned.1.call-start = ((), (), s32[]{:S(2)}) async-start(), calls=%async_computation.3 | async-start | bytes 5242880 | tf_op jit(solution)/shard_map/all_gather | solution.py:39
  89.1 2.0 copy-start.2
  421.3 1.0 copy-start
  422.3 116.5 %all-gather.7.cloned.1.call-start = ((), (), s32[]{:S(2)}) async-start(), calls=%async_computation.2 | async-start | bytes 5242880 | tf_op jit(solution)/shard_map/all_gather | solution.py:40
  429.9 57.7 %copy-start.1 = (f32[1024,256]{1,0:T(8,128)S(1)}, f32[1024,256]{1,0:T(8,128)}, u32[]{:S(2)}) copy-start(f32[1024,256]{1,0:T(8,128)} %copy-done) | copy-start | bytes 3145732
  440.6 1.1 copy-start.3
  441.7 97.2 %copy-start.4 = (f32[1024,256]{1,0:T(8,128)S(1)}, f32[1024,256]{1,0:T(8,128)}, u32[]{:S(2)}) copy-start(f32[1024,256]{1,0:T(8,128)} %copy-done.3) | copy-start | bytes 3145732
  497.7 41.2 %collective-permute-start.1 = (f32[1024,256]{1,0:T(8,128)}, f32[1024,256]{1,0:T(8,128)}, u32[]{:S(2)}, u32[]{:S(2)}) collective-permute-start(f32[1024,256]{1,0:T(8,128)} %convolution_negate_fusion.1), channel_id=1, source_target_pairs={{0,4},{4,8},{8,12},{12,16},{16,20},{20,24},{24,28},{28,32},{32,36}... | collective-permute-start | bytes 3145736 | tf_op jit(solution)/shard_map/ppermute | solution.py:12
  550.4 107.4 %all-to-all-start = ((f32[1,1024,256]{2,0,1:T(1,128)}), f32[1,1024,256]{2,0,1:T(1,128)S(1)}, u32[]{:S(2)}, u32[]{:S(2)}) async-start(f32[1,1024,256]{2,0,1:T(1,128)} %copy.12), calls=%async_computation | async-start | bytes 2097152 | tf_op jit(solution)/shard_map/all_to_all | solution.py:53
  608.8 13.5 %copy-start.6 = (f32[640,64]{0,1:T(8,128)S(1)}, f32[640,64]{0,1:T(8,128)}, u32[]{:S(2)}) copy-start(f32[640,64]{0,1:T(8,128)} %get-tuple-element.131) | copy-start | bytes 491524
  617.4 32.2 %collective-permute-start.2 = (f32[1024,256]{1,0:T(8,128)S(1)}, f32[1024,256]{1,0:T(8,128)S(1)}, u32[]{:S(2)}, u32[]{:S(2)}) collective-permute-start(f32[1024,256]{1,0:T(8,128)S(1)} %convolution_negate_fusion), channel_id=1, source_target_pairs={{0,4},{4,8},{8,12},{12,16},{16,20},{20,24},{24,28},{28,32},{32,36}... | collective-permute-start | bytes 3145736 | tf_op jit(solution)/shard_map/ppermute | solution.py:12
  626.8 465.3 %copy-start.7 = (f32[64,64]{1,0:T(8,128)S(1)}, f32[64,64]{1,0:T(8,128)}, u32[]{:S(2)}) copy-start(f32[64,64]{1,0:T(8,128)} %param.9) | copy-start | bytes 49156
  657.8 441.6 %all-to-all-start.1 = ((f32[1,1024,256]{2,0,1:T(1,128)}), f32[1,1024,256]{2,0,1:T(1,128)}, u32[]{:S(2)}, u32[]{:S(2)}) async-start(f32[1,1024,256]{2,0,1:T(1,128)} %copy.13), calls=%async_computation.1 | async-start | bytes 2097152 | tf_op jit(solution)/shard_map/all_to_all | solution.py:54
  712.1 385.6 %collective-permute-start.3 = (f32[64,256]{1,0:T(8,128)S(1)}, f32[64,256]{1,0:T(8,128)S(1)}, u32[]{:S(2)}, u32[]{:S(2)}) collective-permute-start(f32[64,256]{1,0:T(8,128)S(1)} %convolution_negate_fusion.2), channel_id=1, source_target_pairs={{0,4},{4,8},{8,12},{12,16},{16,20},{20,24},{24,28},{28,32},{32,36}... | collective-permute-start | bytes 196616 | tf_op jit(solution)/shard_map/ppermute | solution.py:12
Sparse Core Ops, SparseCore 0:
  10.2 69.0 all-gather.10
  81.7 65.2 all-gather.12
  422.4 65.1 all-gather.8
  489.3 49.4 all-gather.6
where the time goes:
time: 1120 us; the launch traced here: 1110 us
  blocking collectives  376 us (34%)
  other arithmetic  262 us (23%)
  waiting for transfers between devices  175 us (16%)
  starting transfers between devices  118 us (11%)
  matrix products  108 us (10%)
  local copies, waits for them, and re-layouts  50 us (4%)
  between operations  19.9 us (2%)
    psum x1, blocking collectives, body(): tip_total = lax.psum(tip_part, 'tm')  376 us
    another operation x30, other arithmetic, body(): factor = jnp.linalg.cholesky(whole_pivot)  172 us
    another operation x4, other arithmetic, lower_solve(): return lax.linalg.triangular_solve(factor, rhs, left_side=True, lower=True)  83.4 us
    all_gather x1, waiting for transfers between devices, body(): whole_pivot = lax.all_gather(pivot_strip, 'tile', axis=1, tiled=True)  66.3 us
    all_to_all x1, starting transfers between devices, body(): lax.all_to_all(whole_diag[None], 'tm', split_axis=1, concat_axis=0, tiled...  55.6 us
    another operation x45, matrix products, lower_solve(): return lax.linalg.triangular_solve(factor, rhs, left_side=True, lower=True)  51.3 us
    all_to_all x1, starting transfers between devices, body(): lax.all_to_all(came_upper[None], 'tm', split_axis=1, concat_axis=0, tiled...  48.6 us
    all_gather x1, waiting for transfers between devices, body(): link_all = lax.all_gather(link_strip, 'tile', axis=1, tiled=True)  46 us
  transfers between devices with their start and end apart: 10, of which 5 were waited for; matrix products, arithmetic and copies ran while one was open for 36% of the time, Pallas kernels for 0%

commit v1 on v0

v1 whole, which is shorter than its diff:
```python
import jax
import jax.numpy as jnp
from jax import lax
from jax.sharding import PartitionSpec as P

precise = lax.Precision.HIGHEST


def shifted(value, axis, by):
    count = lax.axis_size(axis)
    pairs = [(i, i + by) for i in range(count) if 0 <= i + by < count]
    return lax.ppermute(value, axis, pairs)


def lower_solve(factor, rhs):
    return lax.linalg.triangular_solve(factor, rhs, left_side=True, lower=True)


def product(left, right):
    return jnp.dot(left.T, right, precision=precise)


def body(diag_blocks, upper_blocks, arrow_blocks, tip_block):
    strip_width = diag_blocks.shape[2]
    offset = lax.axis_index("tile") * strip_width
    upper_after = shifted(upper_blocks[0], "tm", -1)
    both_full = lax.all_gather(
        jnp.stack([diag_blocks[1], upper_blocks[1]]), "tile", axis=2, tiled=True)
    whole_pivot = both_full[0]
    first_full = both_full[1]
    fill_strip = lax.dynamic_slice_in_dim(first_full, offset, strip_width, 0).T
    top_diag = diag_blocks[0]
    top_arrow = arrow_blocks[0].T
    branch_cols = arrow_blocks[1].T
    factor = jnp.linalg.cholesky(whole_pivot)
    branch_solved = lower_solve(factor, branch_cols)
    tip_part = -product(branch_solved, branch_solved)
    tip_all = lax.all_gather(tip_part, "tm")
    fill_solved = lower_solve(factor, fill_strip)
    link_strip = lower_solve(factor, upper_after)
    solved_all = lax.all_gather(
        jnp.stack([link_strip, fill_solved]), "tile", axis=2, tiled=True)
    link_all = solved_all[0]
    fill_all = solved_all[1]
    top_diag = top_diag - product(fill_all, fill_solved)
    top_arrow = top_arrow - product(fill_all, branch_solved)
    next_diag = -product(link_all, link_strip)
    next_upper = -product(fill_all, link_strip)
    next_arrow = -product(branch_solved, link_strip)
    red_tip = tip_block + jnp.sum(tip_all, axis=0)
    own_arrow = lax.dynamic_slice_in_dim(top_arrow, offset, strip_width, 0).T
    came_diag, came_upper, came_arrow = shifted((next_diag, next_upper, next_arrow), "tm", 1)
    whole_diag = top_diag + came_diag
    stacked = jnp.stack([whole_diag, came_upper])[None]
    spread = lax.all_to_all(stacked, "tm", split_axis=2, concat_axis=0, tiled=True)
    red_diag = spread[:, 0]
    red_upper = spread[:, 1]
    red_arrow = (own_arrow + came_arrow)[None]
    return (red_diag, red_upper, red_arrow, red_tip)


def solution(mesh):
    return jax.shard_map(
        body,
        mesh=mesh,
        in_specs=(P("tm", None, "tile"), P("tm", None, "tile"), P("tm", None, None), P()),
        out_specs=(P(None, "tm", "tile"), P(None, "tm", "tile"), P("tm", None, "tile"), P()),
        check_vma=False,
    )
```

time: 1120 us -> 814 us (0.73)
  the two profiles are of different devices: /device:TPU:32 before, /device:TPU:1 now
where the time goes in v1:
time: 814 us; the launch traced here: 809 us
  waiting for transfers between devices  307 us (38%)
  other arithmetic  268 us (33%)
  matrix products  89.5 us (11%)
  starting transfers between devices  70.2 us (9%)
  local copies, waits for them, and re-layouts  55.1 us (7%)
  between operations  19.8 us (2%)
    another operation x30, other arithmetic, body(): factor = jnp.linalg.cholesky(whole_pivot)  173 us
    all_gather x1, waiting for transfers between devices, body(): lax.all_gather(jnp.stack([diag_blocks[1], upper_blocks[1]]), 'tile', axis...  106 us
    all_gather x1, waiting for transfers between devices, body(): lax.all_gather(jnp.stack([link_strip, fill_solved]), 'tile', axis=2, tile...  91.2 us
    all_gather x1, waiting for transfers between devices, body(): tip_all = lax.all_gather(tip_part, 'tm')  87 us
    another operation x4, other arithmetic, lower_solve(): return lax.linalg.triangular_solve(factor, rhs, left_side=True, lower=True)  83.8 us
    all_to_all x1, starting transfers between devices, body(): lax.all_to_all(stacked, 'tm', split_axis=2, concat_axis=0, tiled=True)  59 us
    another operation x45, matrix products, lower_solve(): return lax.linalg.triangular_solve(factor, rhs, left_side=True, lower=True)  35.5 us
    dot_general x6, matrix products, product(): return jnp.dot(left.T, right, precision=precise)  30.7 us
  transfers between devices with their start and end apart: 8, of which 5 were waited for; matrix products, arithmetic and copies ran while one was open for 46% of the time, Pallas kernels for 0%

profile of v1, /device:TPU:1, one launch (start us, length us, event | category | flops | bytes accessed | tf_op | source)
XLA Modules:
  0.0 809.4 jit_solution(15838064834915883190)
XLA Ops:
  8.8 2.6 fusion.148
  14.7 106.1 %all-gather.5.cloned.1.call-done = f32[2,1024,1024]{1,2,0:T(8,128)} async-done(((f32[2,1024,256]{1,2,0:T(8,128)}), f32[2,1024,1024]{1,2,0:T(8,128)}) %all-gather.5.cloned.1.call-update) | async-done | bytes 8388624 | tf_op jit(solution)/shard_map/all_gather | solution.py:27
  120.8 8.4 %fusion.147 = (f32[1,1024,1024]{1,2,0:T(8,128)}, f32[1024,1024]{0,1:T(8,128)}) fusion(f32[2,1024,1024]{1,2,0:T(8,128)} %all-gather.5.cloned.1.call-done), kind=kLoop, calls=%fused_computation.322 | loop fusion | bytes 16777216 | tf_op jit(solution)/shard_map/slice | solution.py:30
  129.2 5.5 copy.13
  134.7 4.4 fusion.1
  141.1 11.7 %cholesky.223 = f32[128,128]{1,0:T(8,128)S(1)} custom-call(f32[128,128]{1,0:T(8,128)S(1)} %cholesky.580), custom_call_target="Cholesky" | custom-call | tf_op jit(solution)/shard_map/jit(cholesky)/cholesky | solution.py:35
  152.9 9.8 %custom-call.65 = f32[1,128,128]{1,2,0:T(8,128)S(1)} custom-call(f32[1,128,128]{2,1,0:T(8,128)S(1)} %get-tuple-element.118), custom_call_target="InvertDiagBlocksLowerTriangular" | custom-call | tf_op jit(solution)/shard_map/jit(cholesky)/cholesky | solution.py:35
  162.7 2.5 cholesky.255
  165.2 2.4 constant_dynamic-update-slice_fusion.79
  169.1 11.9 %cholesky.244 = f32[128,128]{1,0:T(8,128)S(1)} custom-call(f32[128,128]{1,0:T(8,128)S(1)} %cholesky.584), custom_call_target="Cholesky" | custom-call | tf_op jit(solution)/shard_map/jit(cholesky)/cholesky | solution.py:35
  181.7 9.8 %custom-call.66 = f32[1,128,128]{1,2,0:T(8,128)S(1)} custom-call(f32[1,128,128]{2,1,0:T(8,128)S(1)} %get-tuple-element.115), custom_call_target="InvertDiagBlocksLowerTriangular" | custom-call | tf_op jit(solution)/shard_map/jit(cholesky)/cholesky | solution.py:35
  194.8 11.7 %cholesky.468 = f32[128,128]{1,0:T(8,128)S(1)} custom-call(f32[128,128]{1,0:T(8,128)S(1)} %cholesky.589), custom_call_target="Cholesky" | custom-call | tf_op jit(solution)/shard_map/jit(cholesky)/cholesky | solution.py:35
  207.9 9.8 %custom-call.67 = f32[1,128,128]{1,2,0:T(8,128)S(1)} custom-call(f32[1,128,128]{2,1,0:T(8,128)S(1)} %get-tuple-element.112), custom_call_target="InvertDiagBlocksLowerTriangular" | custom-call | tf_op jit(solution)/shard_map/jit(cholesky)/cholesky | solution.py:35
  218.9 2.3 convolution_subtract_fusion.2
  221.2 12.1 %cholesky.487 = f32[128,128]{1,0:T(8,128)S(1)} custom-call(f32[128,128]{1,0:T(8,128)S(1)} %cholesky.594), custom_call_target="Cholesky" | custom-call | tf_op jit(solution)/shard_map/jit(cholesky)/cholesky | solution.py:35
  234.6 9.8 %custom-call.68 = f32[1,128,128]{1,2,0:T(8,128)S(1)} custom-call(f32[1,128,128]{2,1,0:T(8,128)S(1)} %get-tuple-element.109), custom_call_target="InvertDiagBlocksLowerTriangular" | custom-call | tf_op jit(solution)/shard_map/jit(cholesky)/cholesky | solution.py:35
  245.5 2.4 convolution_subtract_fusion.3
  247.9 11.7 %cholesky.506 = f32[128,128]{1,0:T(8,128)S(1)} custom-call(f32[128,128]{1,0:T(8,128)S(1)} %cholesky.599), custom_call_target="Cholesky" | custom-call | tf_op jit(solution)/shard_map/jit(cholesky)/cholesky | solution.py:35
  261.0 9.9 %custom-call.69 = f32[1,128,128]{1,2,0:T(8,128)S(1)} custom-call(f32[1,128,128]{2,1,0:T(8,128)S(1)} %get-tuple-element.106), custom_call_target="InvertDiagBlocksLowerTriangular" | custom-call | tf_op jit(solution)/shard_map/jit(cholesky)/cholesky | solution.py:35
  271.9 2.3 convolution_subtract_fusion.4
  274.2 11.7 %cholesky.526 = f32[128,128]{1,0:T(8,128)S(1)} custom-call(f32[128,128]{1,0:T(8,128)S(1)} %cholesky.604), custom_call_target="Cholesky" | custom-call | tf_op jit(solution)/shard_map/jit(cholesky)/cholesky | solution.py:35
  287.3 9.8 %custom-call.70 = f32[1,128,128]{1,2,0:T(8,128)S(1)} custom-call(f32[1,128,128]{2,1,0:T(8,128)S(1)} %get-tuple-element.103), custom_call_target="InvertDiagBlocksLowerTriangular" | custom-call | tf_op jit(solution)/shard_map/jit(cholesky)/cholesky | solution.py:35
  300.1 11.9 %cholesky.546 = f32[128,128]{1,0:T(8,128)S(1)} custom-call(f32[128,128]{1,0:T(8,128)S(1)} %cholesky.609), custom_call_target="Cholesky" | custom-call | tf_op jit(solution)/shard_map/jit(cholesky)/cholesky | solution.py:35
  313.3 9.8 %custom-call.71 = f32[1,128,128]{1,2,0:T(8,128)S(1)} custom-call(f32[1,128,128]{2,1,0:T(8,128)S(1)} %get-tuple-element.100), custom_call_target="InvertDiagBlocksLowerTriangular" | custom-call | tf_op jit(solution)/shard_map/jit(cholesky)/cholesky | solution.py:35
  325.9 11.7 %cholesky.564 = f32[128,128]{1,0:T(8,128)S(1)} custom-call(f32[128,128]{1,0:T(8,128)S(1)} %convolution_subtract_fusion.13), custom_call_target="Cholesky" | custom-call | tf_op jit(solution)/shard_map/jit(cholesky)/cholesky | solution.py:35
  344.7 4.8 select_select_fusion
  349.5 23.2 %while.5 = (s32[]{:T(128)}, f32[1024,1024]{1,0:T(8,128)}, s32[8,2]{0,1:T(2,128)S(1)}, f32[8,128,128]{2,1,0:T(8,128)S(1)}, s32[]{:T(128)}) while((s32[]{:T(128)}, f32[1024,1024]{1,0:T(8,128)}, s32[8,2]{0,1:T(2,128)S(1)}, f32[8,128,128]{2,1,0:T(8,128)S(1)}, s32[]{:T(128)}) %tuple.117), condition=%wide.while_cond, body=%wide.while_body.sunk | while | flops 2 | bytes 131189 | solution.py:16
  350.1 2.3 bitcast_dynamic-update-slice_fusion.2
  353.0 2.3 bitcast_dynamic-update-slice_fusion.2
  355.9 2.3 bitcast_dynamic-update-slice_fusion.2
  358.8 2.3 bitcast_dynamic-update-slice_fusion.2
  361.7 2.3 bitcast_dynamic-update-slice_fusion.2
  364.6 2.3 bitcast_dynamic-update-slice_fusion.2
  367.5 2.3 bitcast_dynamic-update-slice_fusion.2
  372.7 79.0 %custom-call.74 = f32[8,128,128]{1,2,0:T(8,128)S(1)} custom-call(f32[8,128,128]{2,1,0:T(8,128)S(1)} %get-tuple-element.27), custom_call_target="InvertDiagBlocksLowerTriangular" | custom-call | tf_op jit(solution)/shard_map/triangular_solve/custom-call.7 | solution.py:16
  480.4 91.2 %all-gather.7.cloned.1.call-done = f32[2,1024,1024]{2,1,0:T(8,128)} async-done(((f32[2,1024,256]{2,1,0:T(8,128)}), f32[2,1024,1024]{2,1,0:T(8,128)}) %all-gather.7.cloned.1.call-update) | async-done | bytes 8388624 | tf_op jit(solution)/shard_map/all_gather | solution.py:41
  571.6 8.8 %fusion.9 = f32[1024,256]{1,0:T(8,128)S(1)} fusion(f32[1024,256]{1,0:T(8,128)S(1)} %convolution_dynamic-update-slice_fusion.5, f32[2,1024,1024]{2,1,0:T(8,128)} %all-gather.7.cloned.1.call-done), kind=kOutput, calls=%fused_computation.21 | convolution fusion | flops 3221487616 | bytes 6291456 | tf_op jit(solution)/shard_map/dot_general | solution.py:20
  580.4 3.3 collective-permute-start.1
  583.7 8.5 %fusion.8 = f32[1024,256]{1,0:T(8,128)S(1)} fusion(f32[1024,256]{1,0:T(8,128)S(1)} %convolution_dynamic-update-slice_fusion.5, f32[2,1024,1024]{2,1,0:T(8,128)} %all-gather.7.cloned.1.call-done), kind=kOutput, calls=%fused_computation.20 | convolution fusion | flops 3221487616 | bytes 6291456 | tf_op jit(solution)/shard_map/dot_general | solution.py:20
  592.2 3.3 collective-permute-start.2
  599.2 7.3 collective-permute-done.1
  606.5 6.9 fusion.7
  613.5 15.1 %collective-permute-done.2 = f32[1024,256]{1,0:T(8,128)S(1)} collective-permute-done((f32[1024,256]{1,0:T(8,128)S(1)}, f32[1024,256]{1,0:T(8,128)S(1)}, u32[]{:S(2)}, u32[]{:S(2)}) %collective-permute-start.2) | collective-permute-done | bytes 1048608 | tf_op jit(solution)/shard_map/ppermute | solution.py:12
  628.7 3.0 copy.14
  631.7 59.0 %all-to-all-start = ((f32[1,2,1024,256]{3,1,0,2:T(2,128)}), f32[1,2,1024,256]{3,1,0,2:T(2,128)S(1)}, u32[]{:S(2)}, u32[]{:S(2)}) async-start(f32[1,2,1024,256]{3,1,0,2:T(2,128)} %copy.14), calls=%async_computation | async-start | bytes 4194304 | tf_op jit(solution)/shard_map/all_to_all | solution.py:55
  702.0 2.9 collective-permute-start.3
  704.9 87.0 %all-gather.9.cloned.1.call-done = f32[4096,64]{1,0:T(8,128)} async-done(((f32[64,64]{1,0:T(8,128)}), f32[4096,64]{1,0:T(8,128)}) %all-gather.9.cloned.1.call-update) | async-done | bytes 1048592 | tf_op jit(solution)/shard_map/all_gather | solution.py:38
  794.3 4.9 fusion.2
  (144 shorter events, 86.2 us)
Async XLA Ops:
  7.2 113.7 %all-gather.5.cloned.1.call-start = ((), (), s32[]{:S(2)}) async-start(), calls=%async_computation.1 | async-start | bytes 10485760 | tf_op jit(solution)/shard_map/all_gather | solution.py:27
  13.4 558.2 %all-gather.7.cloned.1.call-start = ((), (), s32[]{:S(2)}) async-start(), calls=%async_computation.2 | async-start | bytes 10485760 | tf_op jit(solution)/shard_map/all_gather | solution.py:41
  13.4 446.0 %collective-permute-start = (f32[1024,256]{1,0:T(8,128)}, f32[1024,256]{1,0:T(8,128)}, u32[]{:S(2)}, u32[]{:S(2)}) collective-permute-start(f32[1024,256]{1,0:T(8,128)} %get-tuple-element.44), channel_id=1, source_target_pairs={{4,0},{8,4},{12,8},{16,12},{20,16},{24,20},{28,24},{32,28},{36,32}... | collective-permute-start | bytes 3145736 | tf_op jit(solution)/shard_map/ppermute | solution.py:12
  139.2 2.0 copy-start.2
  451.7 146.0 %copy-start.3 = (f32[8,128,128]{1,2,0:T(8,128)}, f32[8,128,128]{1,2,0:T(8,128)S(1)}, u32[]{:S(2)}) copy-start(f32[8,128,128]{1,2,0:T(8,128)S(1)} %custom-call.74) | copy-start | bytes 1572868
  451.7 3.3 copy-start.1
  470.4 3.7 copy-start.6
  474.9 121.5 %copy-start.5 = (f32[1024,64]{0,1:T(8,128)}, f32[1024,64]{0,1:T(8,128)S(1)}, u32[]{:S(2)}) copy-start(f32[1024,64]{0,1:T(8,128)S(1)} %get-tuple-element.46) | copy-start | bytes 786436
  477.7 0.7 copy-start.7
  478.4 0.7 copy-start.8
  571.6 34.9 %copy-start = (f32[2,1024,1024]{2,1,0:T(8,128)S(1)}, f32[2,1024,1024]{2,1,0:T(8,128)}, u32[]{:S(2)}) copy-start(f32[2,1024,1024]{2,1,0:T(8,128)} %all-gather.7.cloned.1.call-done) | copy-start | bytes 25165828
  580.4 26.2 %copy-start.4 = (f32[2,1024,256]{2,1,0:T(8,128)S(1)}, f32[2,1024,256]{2,1,0:T(8,128)}, u32[]{:S(2)}) copy-start(f32[2,1024,256]{2,1,0:T(8,128)} %param.6) | copy-start | bytes 6291460
  580.4 26.1 %collective-permute-start.1 = (f32[1024,256]{1,0:T(8,128)S(1)}, f32[1024,256]{1,0:T(8,128)S(1)}, u32[]{:S(2)}, u32[]{:S(2)}) collective-permute-start(f32[1024,256]{1,0:T(8,128)S(1)} %fusion.9), channel_id=1, source_target_pairs={{0,4},{4,8},{8,12},{12,16},{16,20},{20,24},{24,28},{28,32},{32,36}... | collective-permute-start | bytes 3145736 | tf_op jit(solution)/shard_map/ppermute | solution.py:12
  592.2 36.4 %collective-permute-start.2 = (f32[1024,256]{1,0:T(8,128)S(1)}, f32[1024,256]{1,0:T(8,128)S(1)}, u32[]{:S(2)}, u32[]{:S(2)}) collective-permute-start(f32[1024,256]{1,0:T(8,128)S(1)} %fusion.8), channel_id=1, source_target_pairs={{0,4},{4,8},{8,12},{12,16},{16,20},{20,24},{24,28},{28,32},{32,36}... | collective-permute-start | bytes 3145736 | tf_op jit(solution)/shard_map/ppermute | solution.py:12
  598.5 0.7 copy-start.9
  631.7 169.1 %all-to-all-start = ((f32[1,2,1024,256]{3,1,0,2:T(2,128)}), f32[1,2,1024,256]{3,1,0,2:T(2,128)S(1)}, u32[]{:S(2)}, u32[]{:S(2)}) async-start(f32[1,2,1024,256]{3,1,0,2:T(2,128)} %copy.14), calls=%async_computation | async-start | bytes 4194304 | tf_op jit(solution)/shard_map/all_to_all | solution.py:55
  690.7 103.0 %copy-start.10 = (f32[64,64]{1,0:T(8,128)S(1)}, f32[64,64]{1,0:T(8,128)}, u32[]{:S(2)}) copy-start(f32[64,64]{1,0:T(8,128)} %param.9) | copy-start | bytes 49156
  690.7 101.2 %all-gather.9.cloned.1.call-start = ((), (), s32[]{:S(2)}) async-start(), calls=%async_computation.3 | async-start | bytes 2129920 | tf_op jit(solution)/shard_map/all_gather | solution.py:38
  702.0 97.3 %collective-permute-start.3 = (f32[64,256]{1,0:T(8,128)S(1)}, f32[64,256]{1,0:T(8,128)S(1)}, u32[]{:S(2)}, u32[]{:S(2)}) collective-permute-start(f32[64,256]{1,0:T(8,128)S(1)} %convolution_negate_fusion), channel_id=1, source_target_pairs={{0,4},{4,8},{8,12},{12,16},{16,20},{20,24},{24,28},{28,32},{32,36}... | collective-permute-start | bytes 196616 | tf_op jit(solution)/shard_map/ppermute | solution.py:12
Sparse Core Ops, SparseCore 0:
  13.5 107.3 all-gather.4
  474.2 97.2 all-gather.6
  701.5 90.4 all-gather.8

commit v2 on v1

v2 whole, which is shorter than its diff:
```python
import jax
import jax.numpy as jnp
from jax import lax
from jax.sharding import PartitionSpec as P

precise = lax.Precision.HIGHEST
BLOCK = 128


def shifted(value, axis, by):
    count = lax.axis_size(axis)
    pairs = [(i, i + by) for i in range(count) if 0 <= i + by < count]
    return lax.ppermute(value, axis, pairs)


def mm(left, right):
    return jnp.dot(left, right, precision=precise)


def product(left, right):
    return jnp.dot(left.T, right, precision=precise)


def full_columns(strips):
    tile = lax.axis_index("tile")
    count = lax.axis_size("tile")
    far = lax.ppermute(strips, "tile", [(j, j ^ 2) for j in range(count)])
    upper_chip = tile // 2 == 1
    low = jnp.where(upper_chip, far, strips)
    high = jnp.where(upper_chip, strips, far)
    mine = jnp.stack([low, high])
    other = lax.ppermute(mine, "tile", [(j, j ^ 1) for j in range(count)])
    second_core = tile % 2 == 1
    first = jnp.where(second_core, other, mine)
    second = jnp.where(second_core, mine, other)
    return jnp.concatenate([first[0], second[0], first[1], second[1]], axis=-1)


def factor_blocks(pivot):
    size = pivot.shape[0]
    eye = jnp.eye(BLOCK, dtype=pivot.dtype)
    inverses, panels = [], []
    rest = pivot
    for start in range(0, size, BLOCK):
        head = jnp.linalg.cholesky(rest[:BLOCK, :BLOCK])
        head_inv = lax.linalg.triangular_solve(head, eye, left_side=True, lower=True)
        inverses.append(head_inv)
        if start + BLOCK < size:
            below = mm(rest[BLOCK:, :BLOCK], head_inv.T)
            panels.append(below)
            rest = rest[BLOCK:, BLOCK:] - mm(below, below.T)
    return inverses, panels


def forward_solve(inverses, panels, rhs):
    solved = []
    rest = rhs
    for step, head_inv in enumerate(inverses):
        part = mm(head_inv, rest[:BLOCK])
        solved.append(part)
        if step < len(panels):
            rest = rest[BLOCK:] - mm(panels[step], part)
    return jnp.concatenate(solved, axis=0)


def body(diag_blocks, upper_blocks, arrow_blocks, tip_block):
    strip_width = diag_blocks.shape[2]
    nodes = diag_blocks.shape[1]
    offset = lax.axis_index("tile") * strip_width
    upper_after = shifted(upper_blocks[0], "tm", -1)
    whole_pivot = full_columns(diag_blocks[1])
    couplings = full_columns(jnp.stack([upper_blocks[1], upper_after]))
    first_full = couplings[0]
    next_full = couplings[1]
    inverses, panels = factor_blocks(whole_pivot)
    rhs = jnp.concatenate([first_full.T, next_full, arrow_blocks[1].T], axis=1)
    solved = forward_solve(inverses, panels, rhs)
    fill_all = solved[:, :nodes]
    link_all = solved[:, nodes:2 * nodes]
    branch_solved = solved[:, 2 * nodes:]
    tip_part = -product(branch_solved, branch_solved)
    tip_all = lax.all_gather(tip_part, "tm")
    fill_strip = lax.dynamic_slice_in_dim(fill_all, offset, strip_width, 1)
    link_strip = lax.dynamic_slice_in_dim(link_all, offset, strip_width, 1)
    top_diag = diag_blocks[0] - product(fill_all, fill_strip)
    own_arrow = lax.dynamic_slice_in_dim(arrow_blocks[0], offset, strip_width, 1)
    own_arrow = own_arrow - product(branch_solved, fill_strip)
    next_diag = -product(link_all, link_strip)
    next_upper = -product(fill_all, link_strip)
    next_arrow = -product(branch_solved, link_strip)
    red_tip = tip_block + jnp.sum(tip_all, axis=0)
    came_diag, came_upper, came_arrow = shifted((next_diag, next_upper, next_arrow), "tm", 1)
    whole_diag = top_diag + came_diag
    stacked = jnp.stack([whole_diag, came_upper])[None]
    spread = lax.all_to_all(stacked, "tm", split_axis=2, concat_axis=0, tiled=True)
    red_diag = spread[:, 0]
    red_upper = spread[:, 1]
    red_arrow = (own_arrow + came_arrow)[None]
    return (red_diag, red_upper, red_arrow, red_tip)


def solution(mesh):
    return jax.shard_map(
        body,
        mesh=mesh,
        in_specs=(P("tm", None, "tile"), P("tm", None, "tile"), P("tm", None, None), P()),
        out_specs=(P(None, "tm", "tile"), P(None, "tm", "tile"), P("tm", None, "tile"), P()),
        check_vma=False,
    )
```

time: 814 us -> 618 us (0.76)
  waiting for transfers between devices: 307 us -> 177 us
  other arithmetic: 268 us -> 208 us
  starting transfers between devices: 70.2 us -> 103 us
  local copies, waits for them, and re-layouts: 55.1 us -> 34.5 us
  matrix products: 89.5 us -> 75.9 us
    all_gather x2 -> x0, waiting for transfers between devices: 197 us -> none  [the longest x1 106 us: body(): lax.all_gather(jnp.stack([diag_blocks[1], upper_blocks[1]]), 'tile', axis...]
    another operation x36 -> x45, other arithmetic: 259 us -> 195 us  [the longest x24 100 us: factor_blocks(): head = jnp.linalg.cholesky(rest[:BLOCK, :BLOCK])]
    another operation x59 -> x8, matrix products: 58.8 us -> 2.28 us  [factor_blocks(): lax.linalg.triangular_solve(head, eye, left_side=True, lower=True)]
    dot_general x0 -> x29, matrix products: none -> 55.3 us  [mm(): return jnp.dot(left, right, precision=precise)]
    ppermute x4, waiting for transfers between devices: 22.4 us -> 57.9 us  [shifted(): return lax.ppermute(value, axis, pairs)]
    another operation x33 -> x0, local copies, waits for them, and re-layouts: 25.6 us -> none  [the longest x25 23 us: lower_solve(): return lax.linalg.triangular_solve(factor, rhs, left_side=True, lower=True)]
    all_to_all x1, starting transfers between devices: 59 us -> 84 us  [body(): lax.all_to_all(stacked, 'tm', split_axis=2, concat_axis=0, tiled=True)]
    ppermute x0 -> x4, waiting for transfers between devices: none -> 21.8 us  [the longest x2 21.8 us: full_columns(): far = lax.ppermute(strips, 'tile', [(j, j ^ 2) for j in range(count)])]
  transfers between devices with their start and end apart: 8 -> 10, of which waited for: 5 -> 6; matrix products, arithmetic and copies ran while one was open for 46% -> 39% of each run, Pallas kernels for 0% -> 0%
where the time goes in v2:
time: 618 us; the launch traced here: 613 us
  other arithmetic  208 us (34%)
  waiting for transfers between devices  177 us (29%)
  starting transfers between devices  103 us (17%)
  matrix products  75.9 us (12%)
  local copies, waits for them, and re-layouts  34.5 us (6%)
  between operations  15.4 us (2%)
    another operation x24, other arithmetic, factor_blocks(): head = jnp.linalg.cholesky(rest[:BLOCK, :BLOCK])  100 us
    all_gather x1, waiting for transfers between devices, body(): tip_all = lax.all_gather(tip_part, 'tm')  97.4 us
    another operation x16, other arithmetic, factor_blocks(): lax.linalg.triangular_solve(head, eye, left_side=True, lower=True)  84.7 us
    all_to_all x1, starting transfers between devices, body(): lax.all_to_all(stacked, 'tm', split_axis=2, concat_axis=0, tiled=True)  84 us
    ppermute x4, waiting for transfers between devices, shifted(): return lax.ppermute(value, axis, pairs)  57.9 us
    dot_general x29, matrix products, mm(): return jnp.dot(left, right, precision=precise)  55.3 us
    ppermute x2, waiting for transfers between devices, full_columns(): far = lax.ppermute(strips, 'tile', [(j, j ^ 2) for j in range(count)])  21.8 us
    dot_general x6, matrix products, product(): return jnp.dot(left.T, right, precision=precise)  18.3 us
  transfers between devices with their start and end apart: 10, of which 6 were waited for; matrix products, arithmetic and copies ran while one was open for 39% of the time, Pallas kernels for 0%

profile of v2, /device:TPU:1, one launch (start us, length us, event | category | flops | bytes accessed | tf_op | source)
XLA Modules:
  0.0 613.3 jit_solution(18325778737419762282)
XLA Ops:
  8.8 2.6 collective-permute-start
  11.4 21.8 %collective-permute-done = f32[1024,256]{0,1:T(8,128)} collective-permute-done((f32[1024,256]{0,1:T(8,128)S(1)}, f32[1024,256]{0,1:T(8,128)}, u32[]{:S(2)}, u32[]{:S(2)}) %collective-permute-start) | collective-permute-done | bytes 1048608 | tf_op jit(solution)/shard_map/ppermute | solution.py:27
  36.1 2.4 collective-permute-start.1
  43.8 2.3 fusion.95
  46.1 21.8 %collective-permute-done.2 = f32[1024,256]{0,1:T(8,128)} collective-permute-done((f32[1024,256]{0,1:T(8,128)}, f32[1024,256]{0,1:T(8,128)}, u32[]{:S(2)}, u32[]{:S(2)}) %collective-permute-start.2) | collective-permute-done | bytes 1048608 | tf_op jit(solution)/shard_map/ppermute | solution.py:13
  67.9 2.8 pad_maximum_fusion.8
  76.5 11.7 %cholesky.134 = f32[128,128]{1,0:T(8,128)S(1)} custom-call(f32[128,128]{1,0:T(8,128)S(1)} %fusion.85), custom_call_target="Cholesky" | custom-call | tf_op jit(solution)/shard_map/jit(cholesky)/cholesky | solution.py:45
  89.6 9.8 %custom-call.12 = f32[1,128,128]{1,2,0:T(8,128)S(1)} custom-call(f32[1,128,128]{2,1,0:T(8,128)S(1)} %fusion.60), custom_call_target="InvertDiagBlocksLowerTriangular" | custom-call | tf_op jit(solution)/shard_map/triangular_solve/custom-call.0 | solution.py:46
  100.6 4.7 fusion.1
  105.4 12.2 %cholesky.145 = f32[128,128]{1,0:T(8,128)S(1)} custom-call(f32[128,128]{1,0:T(8,128)S(1)} %fusion.83), custom_call_target="Cholesky" | custom-call | tf_op jit(solution)/shard_map/jit(cholesky)/cholesky | solution.py:45
  119.0 9.8 %custom-call.13 = f32[1,128,128]{1,2,0:T(8,128)S(1)} custom-call(f32[1,128,128]{2,1,0:T(8,128)S(1)} %fusion.61), custom_call_target="InvertDiagBlocksLowerTriangular" | custom-call | tf_op jit(solution)/shard_map/triangular_solve/custom-call.0 | solution.py:46
  134.4 11.7 %cholesky.156 = f32[128,128]{1,0:T(8,128)S(1)} custom-call(f32[128,128]{1,0:T(8,128)S(1)} %fusion.81), custom_call_target="Cholesky" | custom-call | tf_op jit(solution)/shard_map/jit(cholesky)/cholesky | solution.py:45
  147.4 10.0 %custom-call.14 = f32[1,128,128]{1,2,0:T(8,128)S(1)} custom-call(f32[1,128,128]{2,1,0:T(8,128)S(1)} %fusion.62), custom_call_target="InvertDiagBlocksLowerTriangular" | custom-call | tf_op jit(solution)/shard_map/triangular_solve/custom-call.0 | solution.py:46
  160.0 2.9 slice_subtract_fusion.2
  163.0 11.7 %cholesky.167 = f32[128,128]{1,0:T(8,128)S(1)} custom-call(f32[128,128]{1,0:T(8,128)S(1)} %fusion.79), custom_call_target="Cholesky" | custom-call | tf_op jit(solution)/shard_map/jit(cholesky)/cholesky | solution.py:45
  176.1 9.8 %custom-call.15 = f32[1,128,128]{1,2,0:T(8,128)S(1)} custom-call(f32[1,128,128]{2,1,0:T(8,128)S(1)} %fusion.63), custom_call_target="InvertDiagBlocksLowerTriangular" | custom-call | tf_op jit(solution)/shard_map/triangular_solve/custom-call.0 | solution.py:46
  189.8 12.1 %cholesky.178 = f32[128,128]{1,0:T(8,128)S(1)} custom-call(f32[128,128]{1,0:T(8,128)S(1)} %fusion.77), custom_call_target="Cholesky" | custom-call | tf_op jit(solution)/shard_map/jit(cholesky)/cholesky | solution.py:45
  203.2 10.4 %custom-call.16 = f32[1,128,128]{1,2,0:T(8,128)} custom-call(f32[1,128,128]{2,1,0:T(8,128)S(1)} %fusion.64), custom_call_target="InvertDiagBlocksLowerTriangular" | custom-call | tf_op jit(solution)/shard_map/triangular_solve/custom-call.0 | solution.py:46
  213.7 2.4 select_bitcast_fusion.1
  216.1 2.3 pad_maximum_fusion.3
  223.8 11.7 %cholesky.189 = f32[128,128]{1,0:T(8,128)S(1)} custom-call(f32[128,128]{1,0:T(8,128)S(1)} %fusion.75), custom_call_target="Cholesky" | custom-call | tf_op jit(solution)/shard_map/jit(cholesky)/cholesky | solution.py:45
  236.9 9.8 %custom-call.17 = f32[1,128,128]{1,2,0:T(8,128)S(1)} custom-call(f32[1,128,128]{2,1,0:T(8,128)S(1)} %fusion.65), custom_call_target="InvertDiagBlocksLowerTriangular" | custom-call | tf_op jit(solution)/shard_map/triangular_solve/custom-call.0 | solution.py:46
  250.4 11.7 %cholesky.200 = f32[128,128]{1,0:T(8,128)S(1)} custom-call(f32[128,128]{1,0:T(8,128)S(1)} %fusion.73), custom_call_target="Cholesky" | custom-call | tf_op jit(solution)/shard_map/jit(cholesky)/cholesky | solution.py:45
  263.4 10.0 %custom-call.18 = f32[1,128,128]{1,2,0:T(8,128)S(1)} custom-call(f32[1,128,128]{2,1,0:T(8,128)S(1)} %fusion.66), custom_call_target="InvertDiagBlocksLowerTriangular" | custom-call | tf_op jit(solution)/shard_map/triangular_solve/custom-call.0 | solution.py:46
  274.4 11.7 %cholesky.211 = f32[128,128]{1,0:T(8,128)S(1)} custom-call(f32[128,128]{1,0:T(8,128)S(1)} %fusion.71), custom_call_target="Cholesky" | custom-call | tf_op jit(solution)/shard_map/jit(cholesky)/cholesky | solution.py:45
  287.4 9.8 %custom-call.19 = f32[1,128,128]{1,2,0:T(8,128)S(1)} custom-call(f32[1,128,128]{2,1,0:T(8,128)S(1)} %fusion.67), custom_call_target="InvertDiagBlocksLowerTriangular" | custom-call | tf_op jit(solution)/shard_map/triangular_solve/custom-call.0 | solution.py:46
  297.5 4.0 broadcast_select_fusion.1
  304.4 4.1 slice_bitcast_fusion.1
  308.5 5.8 copy.31
  314.3 2.4 constant_dynamic-update-slice_fusion.6
  318.1 6.1 fusion
  325.3 5.9 slice_subtract_fusion
  332.3 5.0 convolution_subtract_fusion
  338.3 3.9 convolution_subtract_fusion.1
  343.3 3.0 convolution_subtract_fusion.2
  353.4 3.9 convolution_negate_fusion.1
  357.3 3.5 collective-permute-start.5
  360.8 3.5 convolution_negate_fusion
  364.3 3.2 collective-permute-start.6
  367.5 15.8 %collective-permute-done.5 = f32[1024,256]{1,0:T(8,128)S(1)} collective-permute-done((f32[1024,256]{1,0:T(8,128)S(1)}, f32[1024,256]{1,0:T(8,128)S(1)}, u32[]{:S(2)}, u32[]{:S(2)}) %collective-permute-start.5) | collective-permute-done | bytes 1048608 | tf_op jit(solution)/shard_map/ppermute | solution.py:13
  383.3 3.5 fusion.3
  386.9 18.9 %collective-permute-done.6 = f32[1024,256]{1,0:T(8,128)S(1)} collective-permute-done((f32[1024,256]{1,0:T(8,128)S(1)}, f32[1024,256]{1,0:T(8,128)S(1)}, u32[]{:S(2)}, u32[]{:S(2)}) %collective-permute-start.6) | collective-permute-done | bytes 1048608 | tf_op jit(solution)/shard_map/ppermute | solution.py:13
  405.9 3.0 copy.46
  408.9 84.0 %all-to-all-start = ((f32[1,2,1024,256]{3,1,0,2:T(2,128)}), f32[1,2,1024,256]{3,1,0,2:T(2,128)S(1)}, u32[]{:S(2)}, u32[]{:S(2)}) async-start(f32[1,2,1024,256]{3,1,0,2:T(2,128)} %copy.46), calls=%async_computation | async-start | bytes 4194304 | tf_op jit(solution)/shard_map/all_to_all | solution.py:95
  495.0 2.4 convolution_negate_fusion.2
  497.4 2.9 collective-permute-start.7
  501.6 3.0 fusion.5
  504.6 97.4 %all-gather.3.cloned.1.call-done = f32[4096,64]{1,0:T(8,128)} async-done(((f32[64,64]{1,0:T(8,128)}), f32[4096,64]{1,0:T(8,128)}) %all-gather.3.cloned.1.call-update) | async-done | bytes 1048592 | tf_op jit(solution)/shard_map/all_gather | solution.py:82
  (180 shorter events, 72.7 us)
Async XLA Ops:
  8.8 24.4 %collective-permute-start = (f32[1024,256]{0,1:T(8,128)S(1)}, f32[1024,256]{0,1:T(8,128)}, u32[]{:S(2)}, u32[]{:S(2)}) collective-permute-start(f32[1024,256]{0,1:T(8,128)S(1)} %bitcast.181), channel_id=1, source_target_pairs={{0,2},{1,3},{2,0},{3,1},{4,6},{5,7},{6,4},{7,5},{8,10},{9,11},{10,... | collective-permute-start | bytes 3145736 | tf_op jit(solution)/shard_map/ppermute | solution.py:27
  11.4 27.2 %copy-start.22 = (f32[2,1024,256]{2,1,0:T(8,128)S(1)}, f32[2,1024,256]{2,1,0:T(8,128)}, u32[]{:S(2)}) copy-start(f32[2,1024,256]{2,1,0:T(8,128)} %param.8) | copy-start | bytes 6291460
  36.1 36.3 %collective-permute-start.1 = (f32[2,1024,256]{1,2,0:T(8,128)}, f32[2,1024,256]{1,2,0:T(8,128)}, u32[]{:S(2)}, u32[]{:S(2)}) collective-permute-start(f32[2,1024,256]{1,2,0:T(8,128)} %pad_maximum_fusion.7), channel_id=1, source_target_pairs={{0,1},{1,0},{2,3},{3,2},{4,5},{5,4},{6,7},{7,6},{8,9},{9,8},{10,11... | collective-permute-start | bytes 6291464 | tf_op jit(solution)/shard_map/ppermute | solution.py:32
  40.9 27.0 %collective-permute-start.2 = (f32[1024,256]{0,1:T(8,128)}, f32[1024,256]{0,1:T(8,128)}, u32[]{:S(2)}, u32[]{:S(2)}) collective-permute-start(f32[1024,256]{0,1:T(8,128)} %bitcast.183), channel_id=1, source_target_pairs={{4,0},{8,4},{12,8},{16,12},{20,16},{24,20},{28,24},{32,28},{36,32}... | collective-permute-start | bytes 3145736 | tf_op jit(solution)/shard_map/ppermute | solution.py:13
  43.8 30.9 %copy-start.6 = (f32[1,1024,256]{1,2,0:T(8,128)}, f32[1,1024,256]{1,2,0:T(8,128)S(1)}, u32[]{:S(2)}) copy-start(f32[1,1024,256]{1,2,0:T(8,128)S(1)} %copy.56) | copy-start | bytes 3145732
  70.7 143.0 %collective-permute-start.3 = (f32[2,1024,256]{1,2,0:T(8,128)}, f32[2,1024,256]{1,2,0:T(8,128)}, u32[]{:S(2)}, u32[]{:S(2)}) collective-permute-start(f32[2,1024,256]{1,2,0:T(8,128)} %pad_maximum_fusion.8), channel_id=1, source_target_pairs={{0,2},{1,3},{2,0},{3,1},{4,6},{5,7},{6,4},{7,5},{8,10},{9,11},{10,... | collective-permute-start | bytes 6291464 | tf_op jit(solution)/shard_map/ppermute | solution.py:27
  76.4 24.2 %copy-start.13 = (f32[1024,256]{0,1:T(8,128)}, f32[1024,256]{0,1:T(8,128)S(1)}, u32[]{:S(2)}) copy-start(f32[1024,256]{0,1:T(8,128)S(1)} %get-tuple-element.25) | copy-start | bytes 3145732
  100.6 4.7 copy-start.11
  129.1 4.3 copy-start.32
  129.9 2.1 copy-start.8
  132.0 1.4 copy-start.10
  157.7 0.6 copy-start.34
  162.9 50.8 %copy-start.7 = (f32[1,1024,256]{1,2,0:T(8,128)S(1)}, f32[1,1024,256]{1,2,0:T(8,128)}, u32[]{:S(2)}) copy-start(f32[1,1024,256]{1,2,0:T(8,128)} %copy-done.6) | copy-start | bytes 3145732
  186.2 27.5 %copy-start.24 = (f32[128,128]{1,0:T(8,128)}, f32[128,128]{1,0:T(8,128)S(1)}, u32[]{:S(2)}) copy-start(f32[128,128]{1,0:T(8,128)S(1)} %fusion.45) | copy-start | bytes 196612
  186.8 26.9 %copy-start.14 = (f32[512,128]{1,0:T(8,128)}, f32[512,128]{1,0:T(8,128)S(1)}, u32[]{:S(2)}) copy-start(f32[512,128]{1,0:T(8,128)S(1)} %fusion.35) | copy-start | bytes 786436
  187.8 1.0 copy-start.16
  216.1 2.8 copy-start.5
  216.1 3.8 copy-start.36
  216.1 4.7 copy-start.17
  218.9 78.7 %collective-permute-start.4 = (f32[2,2,1024,256]{2,3,1,0:T(8,128)}, f32[2,2,1024,256]{2,3,1,0:T(8,128)}, u32[]{:S(2)}, u32[]{:S(2)}) collective-permute-start(f32[2,2,1024,256]{2,3,1,0:T(8,128)} %pad_maximum_fusion.3), channel_id=1, source_target_pairs={{0,1},{1,0},{2,3},{3,2},{4,5},{5,4},{6,7},{7,6},{8,9},{9,8},{10,11... | collective-permute-start | bytes 12582920 | tf_op jit(solution)/shard_map/ppermute | solution.py:32
  220.2 0.6 copy-start.26
  221.4 0.7 copy-start.18
  222.0 0.8 copy-start.21
  247.0 0.6 copy-start.28
  273.7 27.9 %copy-start.30 = (f32[128,128]{1,0:T(8,128)}, f32[128,128]{1,0:T(8,128)S(1)}, u32[]{:S(2)}) copy-start(f32[128,128]{1,0:T(8,128)S(1)} %fusion.39) | copy-start | bytes 196612
  308.5 5.8 copy-start.20
  314.3 2.5 copy-start
  314.3 3.8 copy-start.1
  314.3 3.8 copy-start.12
  318.1 6.1 copy-start.33
  324.2 1.0 copy-start.9
  325.3 6.0 copy-start.35
  332.3 5.0 copy-start.25
  337.2 1.0 copy-start.15
  338.3 4.0 copy-start.27
  342.2 1.0 copy-start.19
  343.3 3.0 copy-start.29
  347.4 2.0 copy-start.31
  352.5 8.4 %copy-start.3 = (f32[1024,2112]{0,1:T(8,128)}, f32[1024,2112]{0,1:T(8,128)S(1)}, u32[]{:S(2)}) copy-start(f32[1024,2112]{0,1:T(8,128)S(1)} %convolution_dynamic-update-slice_fusion) | copy-start | bytes 25952260
  353.4 11.0 %copy-start.2 = (f32[1024,1024]{0,1:T(8,128)}, f32[1024,1024]{0,1:T(8,128)S(1)}, u32[]{:S(2)}) copy-start(f32[1024,1024]{0,1:T(8,128)S(1)} %get-tuple-element.7) | copy-start | bytes 12582916
  353.4 30.0 %copy-start.4 = (f32[1024,1024]{0,1:T(8,128)}, f32[1024,1024]{0,1:T(8,128)S(1)}, u32[]{:S(2)}) copy-start(f32[1024,1024]{0,1:T(8,128)S(1)} %get-tuple-element.6) | copy-start | bytes 12582916
  357.3 26.1 %copy-start.23 = (f32[2,1024,256]{2,1,0:T(8,128)S(1)}, f32[2,1024,256]{2,1,0:T(8,128)}, u32[]{:S(2)}) copy-start(f32[2,1024,256]{2,1,0:T(8,128)} %param.7) | copy-start | bytes 6291460
  357.3 26.0 %collective-permute-start.5 = (f32[1024,256]{1,0:T(8,128)S(1)}, f32[1024,256]{1,0:T(8,128)S(1)}, u32[]{:S(2)}, u32[]{:S(2)}) collective-permute-start(f32[1024,256]{1,0:T(8,128)S(1)} %convolution_negate_fusion.1), channel_id=1, source_target_pairs={{0,4},{4,8},{8,12},{12,16},{16,20},{20,24},{24,28},{28,32},{32,36}... | collective-permute-start | bytes 3145736 | tf_op jit(solution)/shard_map/ppermute | solution.py:13
  364.3 41.5 %collective-permute-start.6 = (f32[1024,256]{1,0:T(8,128)S(1)}, f32[1024,256]{1,0:T(8,128)S(1)}, u32[]{:S(2)}, u32[]{:S(2)}) collective-permute-start(f32[1024,256]{1,0:T(8,128)S(1)} %convolution_negate_fusion), channel_id=1, source_target_pairs={{0,4},{4,8},{8,12},{12,16},{16,20},{20,24},{24,28},{28,32},{32,36}... | collective-permute-start | bytes 3145736 | tf_op jit(solution)/shard_map/ppermute | solution.py:13
  408.9 195.5 %all-to-all-start = ((f32[1,2,1024,256]{3,1,0,2:T(2,128)}), f32[1,2,1024,256]{3,1,0,2:T(2,128)S(1)}, u32[]{:S(2)}, u32[]{:S(2)}) async-start(f32[1,2,1024,256]{3,1,0,2:T(2,128)} %copy.46), calls=%async_computation | async-start | bytes 4194304 | tf_op jit(solution)/shard_map/all_to_all | solution.py:95
  492.9 110.9 %copy-start.37 = (f32[64,64]{1,0:T(8,128)S(1)}, f32[64,64]{1,0:T(8,128)}, u32[]{:S(2)}) copy-start(f32[64,64]{1,0:T(8,128)} %param.10) | copy-start | bytes 49156
  492.9 109.1 %all-gather.3.cloned.1.call-start = ((), (), s32[]{:S(2)}) async-start(), calls=%async_computation.1 | async-start | bytes 2129920 | tf_op jit(solution)/shard_map/all_gather | solution.py:82
  497.4 4.2 collective-permute-start.7
Sparse Core Ops, SparseCore 0:
  497.6 104.3 all-gather.2

commit v3 on v2

v3 whole, which is shorter than its diff:
```python
import jax
import jax.numpy as jnp
from jax import lax
from jax.sharding import PartitionSpec as P

precise = lax.Precision.HIGHEST
BLOCK = 128


def shifted(value, axis, by):
    count = lax.axis_size(axis)
    pairs = [(i, i + by) for i in range(count) if 0 <= i + by < count]
    return lax.ppermute(value, axis, pairs)


def mm(left, right):
    return jnp.dot(left, right, precision=precise)


def product(left, right):
    return jnp.dot(left.T, right, precision=precise)


def chip_pair(strips):
    tile = lax.axis_index("tile")
    count = lax.axis_size("tile")
    far = lax.ppermute(strips, "tile", [(j, j ^ 2) for j in range(count)])
    upper_chip = tile // 2 == 1
    low = jnp.where(upper_chip, far, strips)
    high = jnp.where(upper_chip, strips, far)
    return jnp.stack([low, high])


def join_cores(mine):
    tile = lax.axis_index("tile")
    count = lax.axis_size("tile")
    other = lax.ppermute(mine, "tile", [(j, j ^ 1) for j in range(count)])
    second_core = tile % 2 == 1
    first = jnp.where(second_core, other, mine)
    second = jnp.where(second_core, mine, other)
    return jnp.concatenate([first[0], second[0], first[1], second[1]], axis=-1)


def full_columns(strips):
    return join_cores(chip_pair(strips))


def factor_blocks(pivot, riders, hooks):
    size = pivot.shape[0]
    eye = jnp.eye(BLOCK, dtype=pivot.dtype)
    inverses, panels = [], []
    rest = pivot
    for step, start in enumerate(range(0, size, BLOCK)):
        head = jnp.linalg.cholesky(rest[:BLOCK, :BLOCK])
        if step in hooks:
            head, riders = lax.optimization_barrier((head, riders))
            riders = hooks[step](riders)
        head_inv = lax.linalg.triangular_solve(head, eye, left_side=True, lower=True)
        inverses.append(head_inv)
        if start + BLOCK < size:
            below = mm(rest[BLOCK:, :BLOCK], head_inv.T)
            panels.append(below)
            rest = rest[BLOCK:, BLOCK:] - mm(below, below.T)
    return inverses, panels, riders


def forward_solve(inverses, panels, rhs):
    solved = []
    rest = rhs
    for step, head_inv in enumerate(inverses):
        part = mm(head_inv, rest[:BLOCK])
        solved.append(part)
        if step < len(panels):
            rest = rest[BLOCK:] - mm(panels[step], part)
    return jnp.concatenate(solved, axis=0)


def body(diag_blocks, upper_blocks, arrow_blocks, tip_block):
    strip_width = diag_blocks.shape[2]
    nodes = diag_blocks.shape[1]
    parts = lax.axis_size("tm")
    offset = lax.axis_index("tile") * strip_width
    whole_pivot = full_columns(diag_blocks[1])
    hooks = {
        0: lambda r: (chip_pair(r[0]), shifted(r[1], "tm", -1)),
        2: lambda r: (join_cores(r[0]), chip_pair(r[1])),
        4: lambda r: (r[0], join_cores(r[1])),
    }
    inverses, panels, riders = factor_blocks(
        whole_pivot, (upper_blocks[1], upper_blocks[0]), hooks)
    first_full, next_full = riders
    branch_solved = forward_solve(inverses, panels, arrow_blocks[1].T)
    tip_part = -product(branch_solved, branch_solved)
    tip_all = lax.all_gather(tip_part, "tm")
    rhs = jnp.concatenate([first_full.T, next_full], axis=1)
    solved = forward_solve(inverses, panels, rhs)
    fill_all = solved[:, :nodes]
    link_all = solved[:, nodes:]
    fill_strip = lax.dynamic_slice_in_dim(fill_all, offset, strip_width, 1)
    link_strip = lax.dynamic_slice_in_dim(link_all, offset, strip_width, 1)
    top_diag = diag_blocks[0] - product(fill_all, fill_strip)
    own_arrow = lax.dynamic_slice_in_dim(arrow_blocks[0], offset, strip_width, 1)
    own_arrow = own_arrow - product(branch_solved, fill_strip)
    next_arrow = -product(branch_solved, link_strip)
    came_arrow = shifted(next_arrow, "tm", 1)
    next_diag = -product(link_all, link_strip)
    next_upper = -product(fill_all, link_strip)
    stacked = jnp.stack([top_diag, next_diag, next_upper])[None]
    tip_all, stacked = lax.optimization_barrier((tip_all, stacked))
    spread = lax.all_to_all(stacked, "tm", split_axis=2, concat_axis=0, tiled=True)
    zero = jnp.zeros_like(spread[:1, 1])
    before = jnp.concatenate([zero, spread[:parts - 1, 1]], axis=0)
    red_diag = spread[:, 0] + before
    red_upper = jnp.concatenate([zero, spread[:parts - 1, 2]], axis=0)
    red_tip = tip_block + jnp.sum(tip_all, axis=0)
    red_arrow = (own_arrow + came_arrow)[None]
    return (red_diag, red_upper, red_arrow, red_tip)


def solution(mesh):
    return jax.shard_map(
        body,
        mesh=mesh,
        in_specs=(P("tm", None, "tile"), P("tm", None, "tile"), P("tm", None, None), P()),
        out_specs=(P(None, "tm", "tile"), P(None, "tm", "tile"), P("tm", None, "tile"), P()),
        check_vma=False,
    )
```

time: 618 us -> 555 us (0.90)
  starting transfers between devices: 103 us -> 32.1 us
  waiting for transfers between devices: 177 us -> 125 us
  matrix products: 75.9 us -> 101 us
  local copies, waits for them, and re-layouts: 34.5 us -> 51.9 us
  other arithmetic: 208 us -> 219 us
    all_gather x1, waiting for transfers between devices: 97.4 us -> 21.2 us  [body(): tip_all = lax.all_gather(tip_part, 'tm')]
    all_to_all x1, waiting for transfers between devices: 0.01 us -> 66.2 us  [body(): lax.all_to_all(stacked, 'tm', split_axis=2, concat_axis=0, tiled=True)]
    all_to_all x1, starting transfers between devices: 84 us -> 19.5 us  [body(): lax.all_to_all(stacked, 'tm', split_axis=2, concat_axis=0, tiled=True)]
    ppermute x4 -> x2, waiting for transfers between devices: 57.9 us -> 16.2 us  [shifted(): return lax.ppermute(value, axis, pairs)]
    dot_general x29 -> x44, matrix products: 55.3 us -> 70.5 us  [mm(): return jnp.dot(left, right, precision=precise)]
    transpose x2 -> x0, local copies, waits for them, and re-layouts: 9.84 us -> none  [body(): rhs = jnp.concatenate([first_full.T, next_full, arrow_blocks[1].T], axis=1)]
    squeeze x3 -> x10, local copies, waits for them, and re-layouts: 4.86 us -> 14.5 us  [the longest x9 14.3 us: join_cores(): return jnp.concatenate([first[0], second[0], first[1], second[1]], axis=-1)]
    dot_general x6, matrix products: 18.3 us -> 27.1 us  [product(): return jnp.dot(left.T, right, precision=precise)]
  transfers between devices with their start and end apart: 10 -> 10, of which waited for: 6 -> 4; matrix products, arithmetic and copies ran while one was open for 39% -> 61% of each run, Pallas kernels for 0% -> 0%
where the time goes in v3:
time: 555 us; the launch traced here: 545 us
  other arithmetic  219 us (39%)
  waiting for transfers between devices  125 us (23%)
  matrix products  101 us (18%)
  local copies, waits for them, and re-layouts  51.9 us (9%)
  starting transfers between devices  32.1 us (6%)
  between operations  15.3 us (3%)
    another operation x24, other arithmetic, factor_blocks(): head = jnp.linalg.cholesky(rest[:BLOCK, :BLOCK])  102 us
    another operation x16, other arithmetic, factor_blocks(): lax.linalg.triangular_solve(head, eye, left_side=True, lower=True)  86.2 us
    dot_general x44, matrix products, mm(): return jnp.dot(left, right, precision=precise)  70.5 us
    all_to_all x1, waiting for transfers between devices, body(): lax.all_to_all(stacked, 'tm', split_axis=2, concat_axis=0, tiled=True)  66.2 us
    dot_general x6, matrix products, product(): return jnp.dot(left.T, right, precision=precise)  27.1 us
    ppermute x3, waiting for transfers between devices, chip_pair(): far = lax.ppermute(strips, 'tile', [(j, j ^ 2) for j in range(count)])  21.8 us
    all_gather x1, waiting for transfers between devices, body(): tip_all = lax.all_gather(tip_part, 'tm')  21.2 us
    all_to_all x1, starting transfers between devices, body(): lax.all_to_all(stacked, 'tm', split_axis=2, concat_axis=0, tiled=True)  19.5 us
  transfers between devices with their start and end apart: 10, of which 4 were waited for; matrix products, arithmetic and copies ran while one was open for 61% of the time, Pallas kernels for 0%

profile of v3, /device:TPU:1, one launch (start us, length us, event | category | flops | bytes accessed | tf_op | source)
XLA Modules:
  0.0 544.9 jit_solution(7073078359359624474)
XLA Ops:
  8.8 2.6 collective-permute-start
  11.4 21.8 %collective-permute-done = f32[1024,256]{0,1:T(8,128)} collective-permute-done((f32[1024,256]{0,1:T(8,128)S(1)}, f32[1024,256]{0,1:T(8,128)}, u32[]{:S(2)}, u32[]{:S(2)}) %collective-permute-start) | collective-permute-done | bytes 1048608 | tf_op jit(solution)/shard_map/ppermute | solution.py:27
  36.2 2.4 collective-permute-start.1
  38.6 2.6 fusion.99
  41.2 2.6 copy.110
  47.0 2.2 broadcast_select_fusion.4
  51.1 11.7 %cholesky.134 = f32[128,128]{1,0:T(8,128)S(1)} custom-call(f32[128,128]{1,0:T(8,128)S(1)} %fusion.76), custom_call_target="Cholesky" | custom-call | tf_op jit(solution)/shard_map/jit(cholesky)/cholesky | solution.py:54
  66.0 9.8 %custom-call.12 = f32[1,128,128]{1,2,0:T(8,128)S(1)} custom-call(f32[1,128,128]{2,1,0:T(8,128)S(1)} %select_bitcast_fusion.8), custom_call_target="InvertDiagBlocksLowerTriangular" | custom-call | tf_op jit(solution)/shard_map/triangular_solve/custom-call.0 | solution.py:58
  77.8 4.5 fusion
  82.5 11.7 %cholesky.145 = f32[128,128]{1,0:T(8,128)S(1)} custom-call(f32[128,128]{1,0:T(8,128)S(1)} %fusion.74), custom_call_target="Cholesky" | custom-call | tf_op jit(solution)/shard_map/jit(cholesky)/cholesky | solution.py:54
  95.6 9.8 %custom-call.13 = f32[1,128,128]{1,2,0:T(8,128)S(1)} custom-call(f32[1,128,128]{2,1,0:T(8,128)S(1)} %fusion.54), custom_call_target="InvertDiagBlocksLowerTriangular" | custom-call | tf_op jit(solution)/shard_map/triangular_solve/custom-call.0 | solution.py:58
  111.4 11.7 %cholesky.156 = f32[128,128]{1,0:T(8,128)S(1)} custom-call(f32[128,128]{1,0:T(8,128)S(1)} %fusion.72), custom_call_target="Cholesky" | custom-call | tf_op jit(solution)/shard_map/jit(cholesky)/cholesky | solution.py:54
  133.7 16.2 %collective-permute-done.3 = f32[1024,256]{0,1:T(8,128)} collective-permute-done((f32[1024,256]{0,1:T(8,128)}, f32[1024,256]{0,1:T(8,128)}, u32[]{:S(2)}, u32[]{:S(2)}) %collective-permute-start.3) | collective-permute-done | bytes 1048608 | tf_op jit(solution)/shard_map/ppermute | solution.py:13
  151.4 9.8 %custom-call.14 = f32[1,128,128]{1,2,0:T(8,128)S(1)} custom-call(f32[1,128,128]{2,1,0:T(8,128)S(1)} %select_bitcast_fusion.7), custom_call_target="InvertDiagBlocksLowerTriangular" | custom-call | tf_op jit(solution)/shard_map/triangular_solve/custom-call.0 | solution.py:58
  165.9 11.7 %cholesky.167 = f32[128,128]{1,0:T(8,128)S(1)} custom-call(f32[128,128]{1,0:T(8,128)S(1)} %fusion.70), custom_call_target="Cholesky" | custom-call | tf_op jit(solution)/shard_map/jit(cholesky)/cholesky | solution.py:54
  178.9 9.8 %custom-call.15 = f32[1,128,128]{1,2,0:T(8,128)S(1)} custom-call(f32[1,128,128]{2,1,0:T(8,128)S(1)} %fusion.55), custom_call_target="InvertDiagBlocksLowerTriangular" | custom-call | tf_op jit(solution)/shard_map/triangular_solve/custom-call.0 | solution.py:58
  190.6 2.2 convolution_subtract_fusion.3
  193.3 11.7 %cholesky.178 = f32[128,128]{1,0:T(8,128)S(1)} custom-call(f32[128,128]{1,0:T(8,128)S(1)} %fusion.68), custom_call_target="Cholesky" | custom-call | tf_op jit(solution)/shard_map/jit(cholesky)/cholesky | solution.py:54
  210.5 2.7 broadcast_select_fusion.3
  213.4 2.6 pad_maximum_fusion
  216.0 9.8 %custom-call.16 = f32[1,128,128]{1,2,0:T(8,128)S(1)} custom-call(f32[1,128,128]{2,1,0:T(8,128)S(1)} %select_bitcast_fusion.6), custom_call_target="InvertDiagBlocksLowerTriangular" | custom-call | tf_op jit(solution)/shard_map/triangular_solve/custom-call.0 | solution.py:58
  231.0 11.7 %cholesky.189 = f32[128,128]{1,0:T(8,128)S(1)} custom-call(f32[128,128]{1,0:T(8,128)S(1)} %fusion.66), custom_call_target="Cholesky" | custom-call | tf_op jit(solution)/shard_map/jit(cholesky)/cholesky | solution.py:54
  244.1 9.8 %custom-call.17 = f32[1,128,128]{1,2,0:T(8,128)S(1)} custom-call(f32[1,128,128]{2,1,0:T(8,128)S(1)} %fusion.56), custom_call_target="InvertDiagBlocksLowerTriangular" | custom-call | tf_op jit(solution)/shard_map/triangular_solve/custom-call.0 | solution.py:58
  260.6 12.7 %cholesky.200 = f32[128,128]{1,0:T(8,128)S(1)} custom-call(f32[128,128]{1,0:T(8,128)} %fusion.64), custom_call_target="Cholesky" | custom-call | tf_op jit(solution)/shard_map/jit(cholesky)/cholesky | solution.py:54
  275.3 10.6 %custom-call.18 = f32[1,128,128]{1,2,0:T(8,128)S(1)} custom-call(f32[1,128,128]{2,1,0:T(8,128)} %fusion.57), custom_call_target="InvertDiagBlocksLowerTriangular" | custom-call | tf_op jit(solution)/shard_map/triangular_solve/custom-call.0 | solution.py:58
  292.8 13.2 %cholesky.211 = f32[128,128]{1,0:T(8,128)} custom-call(f32[128,128]{1,0:T(8,128)} %fusion.62), custom_call_target="Cholesky" | custom-call | tf_op jit(solution)/shard_map/jit(cholesky)/cholesky | solution.py:54
  309.6 11.3 %custom-call.19 = f32[1,128,128]{1,2,0:T(8,128)} custom-call(f32[1,128,128]{2,1,0:T(8,128)} %fusion.58), custom_call_target="InvertDiagBlocksLowerTriangular" | custom-call | tf_op jit(solution)/shard_map/triangular_solve/custom-call.0 | solution.py:58
  327.9 4.9 bitcast_dynamic-update-slice_fusion
  332.8 3.4 broadcast_select_fusion
  337.6 2.5 copy.96
  343.3 2.6 copy.98
  346.0 2.5 copy.99
  353.0 2.2 constant_dynamic-update-slice_fusion.17
  355.3 8.2 %slice_subtract_fusion = f32[896,2048]{1,0:T(8,128)S(1)} fusion(f32[1024,2048]{1,0:T(8,128)} %constant_dynamic-update-slice_fusion.7, f32[896,128]{1,0:T(8,128)S(1)} %copy-done.3, f32[128,2048]{1,0:T(8,128)S(1)} %get-tuple-element.75), kind=kOutput, calls=%fused_computation | convolution fusion | flops 2820407296 | bytes 16187392 | tf_op jit(solution)/shard_map/dot_general | solution.py:17
  364.5 5.1 slice_subtract_fusion.1
  370.6 4.5 slice_subtract_fusion.2
  376.2 3.8 slice_subtract_fusion.3
  381.0 2.7 slice_subtract_fusion.4
  391.6 6.9 %fusion.2 = f32[1,1024,256]{2,1,0:T(8,128)S(1)} fusion(f32[1024,1024]{1,0:T(8,128)S(1)} %get-tuple-element.29, s32[]{:T(128)S(6)} %select_n.97), kind=kOutput, calls=%fused_computation.23 | convolution fusion | flops 3221487616 | bytes 6291460 | tf_op jit(solution)/shard_map/dot_general | solution.py:21
  398.5 7.3 %fusion.1 = f32[1,1024,256]{2,1,0:T(8,128)S(1)} fusion(f32[1024,1024]{1,0:T(8,128)S(1)} %get-tuple-element.29, s32[]{:T(128)S(6)} %select_n.97, f32[1024,2048]{1,0:T(8,128)S(1)} %convolution_dynamic-update-slice_fusion), kind=kOutput, calls=%fused_computation.21 | convolution fusion | flops 3221487616 | bytes 6291460 | tf_op jit(solution)/shard_map/dot_general | solution.py:21
  405.8 6.9 %fusion.3 = f32[1,1024,256]{2,1,0:T(8,128)S(1)} fusion(f32[1024,1024]{1,0:T(8,128)S(1)} %get-tuple-element.28, f32[2,1024,256]{2,1,0:T(8,128)S(1)} %copy-done.16, s32[]{:T(128)S(6)} %select_n.97), kind=kOutput, calls=%fused_computation.25 | convolution fusion | flops 3221487616 | bytes 7340036 | tf_op jit(solution)/shard_map/dot_general | solution.py:21
  412.9 21.2 %all-gather.3.cloned.1.call-done = f32[4096,64]{1,0:T(8,128)} async-done(((f32[64,64]{1,0:T(8,128)}), f32[4096,64]{1,0:T(8,128)}) %all-gather.3.cloned.1.call-update) | async-done | bytes 1048592 | tf_op jit(solution)/shard_map/all_gather | solution.py:94
  434.1 5.1 copy.100
  439.2 19.5 %all-to-all-start = ((f32[1,3,1024,256]{3,0,1,2:T(1,128)}), f32[1,3,1024,256]{3,0,1,2:T(1,128)S(1)}, u32[]{:S(2)}, u32[]{:S(2)}) async-start(f32[1,3,1024,256]{3,0,1,2:T(1,128)} %copy.100), calls=%async_computation | async-start | bytes 6291456 | tf_op jit(solution)/shard_map/all_to_all | solution.py:110
  458.8 2.5 convolution_negate_fusion.2
  461.3 2.9 collective-permute-start.7
  466.6 2.5 fusion.5
  469.1 66.2 %all-to-all-done = f32[1,3,1024,256]{3,0,1,2:T(1,128)S(1)} async-done(((f32[1,3,1024,256]{3,0,1,2:T(1,128)}), f32[1,3,1024,256]{3,0,1,2:T(1,128)S(1)}, u32[]{:S(2)}, u32[]{:S(2)}) %all-to-all-start) | async-done | bytes 3145760 | tf_op jit(solution)/shard_map/all_to_all | solution.py:110
  (194 shorter events, 106.9 us)
Async XLA Ops:
  7.2 427.0 %all-gather.3.cloned.1.call-start = ((), (), s32[]{:S(2)}) async-start(), calls=%async_computation.1 | async-start | bytes 2129920 | tf_op jit(solution)/shard_map/all_gather | solution.py:94
  8.8 24.4 %collective-permute-start = (f32[1024,256]{0,1:T(8,128)S(1)}, f32[1024,256]{0,1:T(8,128)}, u32[]{:S(2)}, u32[]{:S(2)}) collective-permute-start(f32[1024,256]{0,1:T(8,128)S(1)} %bitcast.222), channel_id=1, source_target_pairs={{0,2},{1,3},{2,0},{3,1},{4,6},{5,7},{6,4},{7,5},{8,10},{9,11},{10,... | collective-permute-start | bytes 3145736 | tf_op jit(solution)/shard_map/ppermute | solution.py:27
  36.2 10.9 %collective-permute-start.1 = (f32[2,1024,256]{1,2,0:T(8,128)}, f32[2,1024,256]{1,2,0:T(8,128)}, u32[]{:S(2)}, u32[]{:S(2)}) collective-permute-start(f32[2,1024,256]{1,2,0:T(8,128)} %pad_maximum_fusion.4), channel_id=1, source_target_pairs={{0,1},{1,0},{2,3},{3,2},{4,5},{5,4},{6,7},{7,6},{8,9},{9,8},{10,11... | collective-permute-start | bytes 6291464 | tf_op jit(solution)/shard_map/ppermute | solution.py:37
  51.0 26.1 %copy-start.9 = (f32[1024,256]{0,1:T(8,128)}, f32[1024,256]{0,1:T(8,128)S(1)}, u32[]{:S(2)}) copy-start(f32[1024,256]{0,1:T(8,128)S(1)} %get-tuple-element.53) | copy-start | bytes 3145732
  64.2 66.2 %collective-permute-start.2 = (f32[1024,256]{0,1:T(8,128)}, f32[1024,256]{0,1:T(8,128)}, u32[]{:S(2)}, u32[]{:S(2)}) collective-permute-start(f32[1024,256]{0,1:T(8,128)} %bitcast.5), channel_id=1, source_target_pairs={{0,2},{1,3},{2,0},{3,1},{4,6},{5,7},{6,4},{7,5},{8,10},{9,11},{10,... | collective-permute-start | bytes 3145736 | tf_op jit(solution)/shard_map/ppermute | solution.py:27
  76.1 48.3 %copy-start.24 = (f32[128,128]{1,0:T(8,128)}, f32[128,128]{1,0:T(8,128)S(1)}, u32[]{:S(2)}) copy-start(f32[128,128]{1,0:T(8,128)S(1)} %fusion.48) | copy-start | bytes 196612
  77.1 0.8 copy-start.2
  106.2 24.1 %copy-start.20 = (f32[128,128]{1,0:T(8,128)}, f32[128,128]{1,0:T(8,128)S(1)}, u32[]{:S(2)}) copy-start(f32[128,128]{1,0:T(8,128)S(1)} %fusion.46) | copy-start | bytes 196612
  107.0 2.1 copy-start.4
  109.1 1.4 copy-start.6
  123.2 26.7 %collective-permute-start.3 = (f32[1024,256]{0,1:T(8,128)}, f32[1024,256]{0,1:T(8,128)}, u32[]{:S(2)}, u32[]{:S(2)}) collective-permute-start(f32[1024,256]{0,1:T(8,128)} %bitcast.224), channel_id=1, source_target_pairs={{4,0},{8,4},{12,8},{16,12},{20,16},{24,20},{28,24},{32,28},{36,32}... | collective-permute-start | bytes 3145736 | tf_op jit(solution)/shard_map/ppermute | solution.py:13
  130.3 31.2 %copy-start.7 = (f32[768,768]{0,1:T(8,128)S(1)}, f32[768,768]{0,1:T(8,128)}, u32[]{:S(2)}) copy-start(f32[768,768]{0,1:T(8,128)} %copy-done.6) | copy-start | bytes 7077892
  149.9 58.6 %collective-permute-start.5 = (f32[1024,256]{0,1:T(8,128)}, f32[1024,256]{0,1:T(8,128)}, u32[]{:S(2)}, u32[]{:S(2)}) collective-permute-start(f32[1024,256]{0,1:T(8,128)} %collective-permute-done.3), channel_id=1, source_target_pairs={{0,2},{1,3},{2,0},{3,1},{4,6},{5,7},{6,4},{7,5},{8,10},{9,11},{10,... | collective-permute-start | bytes 3145736 | tf_op jit(solution)/shard_map/ppermute | solution.py:27
  149.9 60.6 %collective-permute-start.4 = (f32[2,1024,256]{1,2,0:T(8,128)}, f32[2,1024,256]{1,2,0:T(8,128)}, u32[]{:S(2)}, u32[]{:S(2)}) collective-permute-start(f32[2,1024,256]{1,2,0:T(8,128)} %pad_maximum_fusion.5), channel_id=1, source_target_pairs={{0,1},{1,0},{2,3},{3,2},{4,5},{5,4},{6,7},{7,6},{8,9},{9,8},{10,11... | collective-permute-start | bytes 6291464 | tf_op jit(solution)/shard_map/ppermute | solution.py:37
  161.6 44.8 %copy-start.22 = (f32[128,128]{1,0:T(8,128)}, f32[128,128]{1,0:T(8,128)S(1)}, u32[]{:S(2)}) copy-start(f32[128,128]{1,0:T(8,128)S(1)} %fusion.44) | copy-start | bytes 196612
  163.7 1.2 copy-start.10
  192.8 17.4 %copy-start.14 = (f32[512,512]{0,1:T(8,128)}, f32[512,512]{0,1:T(8,128)S(1)}, u32[]{:S(2)}) copy-start(f32[512,512]{0,1:T(8,128)S(1)} %convolution_subtract_fusion.3) | copy-start | bytes 3145732
  216.0 116.8 %collective-permute-start.6 = (f32[2,1024,256]{1,2,0:T(8,128)S(1)}, f32[2,1024,256]{1,2,0:T(8,128)}, u32[]{:S(2)}, u32[]{:S(2)}) collective-permute-start(f32[2,1024,256]{1,2,0:T(8,128)S(1)} %pad_maximum_fusion.6), channel_id=1, source_target_pairs={{0,1},{1,0},{2,3},{3,2},{4,5},{5,4},{6,7},{7,6},{8,9},{9,8},{10,11... | collective-permute-start | bytes 6291464 | tf_op jit(solution)/shard_map/ppermute | solution.py:37
  229.3 0.8 copy-start.15
  256.8 0.7 copy-start.17
  286.2 0.6 copy-start.18
  323.1 3.8 copy-start.26
  336.2 4.0 copy-start.8
  341.7 6.8 %copy-start.11 = (f32[1024,256]{1,0:T(8,128)S(1)}, f32[1024,256]{1,0:T(8,128)}, u32[]{:S(2)}) copy-start(f32[1024,256]{1,0:T(8,128)} %copy.96) | copy-start | bytes 3145732
  348.5 2.3 copy-start.12
  348.5 3.4 copy-start.13
  348.5 4.5 copy-start.25
  350.8 4.5 copy-start.3
  355.3 8.2 %copy-start.21 = (f32[128,128]{1,0:T(8,128)S(1)}, f32[128,128]{1,0:T(8,128)}, u32[]{:S(2)}) copy-start(f32[128,128]{1,0:T(8,128)} %copy-done.20) | copy-start | bytes 196612
  355.3 9.2 %copy-start.5 = (f32[768,128]{1,0:T(8,128)S(1)}, f32[768,128]{1,0:T(8,128)}, u32[]{:S(2)}) copy-start(f32[768,128]{1,0:T(8,128)} %copy-done.4) | copy-start | bytes 1179652
  364.5 5.1 copy-start.23
  383.7 2.9 copy-start.19
  386.6 2.1 copy-start.27
  391.6 14.2 %copy-start = (f32[1024,1024]{1,0:T(8,128)}, f32[1024,1024]{1,0:T(8,128)S(1)}, u32[]{:S(2)}) copy-start(f32[1024,1024]{1,0:T(8,128)S(1)} %get-tuple-element.29) | copy-start | bytes 12582916
  391.6 14.2 %copy-start.1 = (f32[1024,1024]{1,0:T(8,128)}, f32[1024,1024]{1,0:T(8,128)S(1)}, u32[]{:S(2)}) copy-start(f32[1024,1024]{1,0:T(8,128)S(1)} %get-tuple-element.28) | copy-start | bytes 12582916
  398.5 7.3 %copy-start.16 = (f32[2,1024,256]{2,1,0:T(8,128)S(1)}, f32[2,1024,256]{2,1,0:T(8,128)}, u32[]{:S(2)}) copy-start(f32[2,1024,256]{2,1,0:T(8,128)} %param.7) | copy-start | bytes 6291460
  439.2 26.7 %copy-start.28 = (f32[64,64]{1,0:T(8,128)S(1)}, f32[64,64]{1,0:T(8,128)}, u32[]{:S(2)}) copy-start(f32[64,64]{1,0:T(8,128)} %param.10) | copy-start | bytes 49156
  439.2 96.0 %all-to-all-start = ((f32[1,3,1024,256]{3,0,1,2:T(1,128)}), f32[1,3,1024,256]{3,0,1,2:T(1,128)S(1)}, u32[]{:S(2)}, u32[]{:S(2)}) async-start(f32[1,3,1024,256]{3,0,1,2:T(1,128)} %copy.100), calls=%async_computation | async-start | bytes 6291456 | tf_op jit(solution)/shard_map/all_to_all | solution.py:110
  461.3 5.3 collective-permute-start.7
Sparse Core Ops, SparseCore 0:
  328.0 106.0 all-gather.2

commit v4 on v3

--- a/solution.py
+++ b/solution.py
@@ -81,13 +81,13 @@
     parts = lax.axis_size("tm")
     offset = lax.axis_index("tile") * strip_width
     whole_pivot = full_columns(diag_blocks[1])
+    upper_after = shifted(upper_blocks[0], "tm", -1)
     hooks = {
-        0: lambda r: (chip_pair(r[0]), shifted(r[1], "tm", -1)),
-        2: lambda r: (join_cores(r[0]), chip_pair(r[1])),
-        4: lambda r: (r[0], join_cores(r[1])),
+        0: lambda r: (chip_pair(r[0]), chip_pair(r[1])),
+        3: lambda r: (join_cores(r[0]), join_cores(r[1])),
     }
     inverses, panels, riders = factor_blocks(
-        whole_pivot, (upper_blocks[1], upper_blocks[0]), hooks)
+        whole_pivot, (upper_blocks[1], upper_after), hooks)
     first_full, next_full = riders
     branch_solved = forward_solve(inverses, panels, arrow_blocks[1].T)
     tip_part = -product(branch_solved, branch_solved)
@@ -106,7 +106,7 @@
     next_diag = -product(link_all, link_strip)
     next_upper = -product(fill_all, link_strip)
     stacked = jnp.stack([top_diag, next_diag, next_upper])[None]
-    tip_all, stacked = lax.optimization_barrier((tip_all, stacked))
+    tip_all, came_arrow, stacked = lax.optimization_barrier((tip_all, came_arrow, stacked))
     spread = lax.all_to_all(stacked, "tm", split_axis=2, concat_axis=0, tiled=True)
     zero = jnp.zeros_like(spread[:1, 1])
     before = jnp.concatenate([zero, spread[:parts - 1, 1]], axis=0)

time: 555 us -> 579 us (1.043)
  other arithmetic: 219 us -> 239 us
  matrix products: 101 us -> 111 us
    ppermute x2, waiting for transfers between devices: 16.2 us -> 5.37 us  [shifted(): return lax.ppermute(value, axis, pairs)]
    another operation x16, other arithmetic: 86.2 us -> 96.4 us  [factor_blocks(): lax.linalg.triangular_solve(head, eye, left_side=True, lower=True)]
    another operation x24, other arithmetic: 102 us -> 110 us  [factor_blocks(): head = jnp.linalg.cholesky(rest[:BLOCK, :BLOCK])]
    dot_general x44, matrix products: 70.5 us -> 77.2 us  [mm(): return jnp.dot(left, right, precision=precise)]
    slice x14, local copies, waits for them, and re-layouts: 2.53 us -> 8.41 us  [factor_blocks(): head = jnp.linalg.cholesky(rest[:BLOCK, :BLOCK])]
    unnamed x65 -> x90, local copies, waits for them, and re-layouts: 18.1 us -> 14.1 us
  transfers between devices with their start and end apart: 10 -> 10, of which waited for: 4 -> 4; matrix products, arithmetic and copies ran while one was open for 61% -> 66% of each run, Pallas kernels for 0% -> 0%
where the time goes in v4:
time: 579 us; the launch traced here: 570 us
  other arithmetic  239 us (41%)
  waiting for transfers between devices  121 us (21%)
  matrix products  111 us (19%)
  local copies, waits for them, and re-layouts  52.2 us (9%)
  starting transfers between devices  31.3 us (5%)
  between operations  15.6 us (3%)
    another operation x24, other arithmetic, factor_blocks(): head = jnp.linalg.cholesky(rest[:BLOCK, :BLOCK])  110 us
    another operation x16, other arithmetic, factor_blocks(): lax.linalg.triangular_solve(head, eye, left_side=True, lower=True)  96.4 us
    dot_general x44, matrix products, mm(): return jnp.dot(left, right, precision=precise)  77.2 us
    all_to_all x1, waiting for transfers between devices, body(): lax.all_to_all(stacked, 'tm', split_axis=2, concat_axis=0, tiled=True)  71.8 us
    dot_general x6, matrix products, product(): return jnp.dot(left.T, right, precision=precise)  26.7 us
    all_gather x1, waiting for transfers between devices, body(): tip_all = lax.all_gather(tip_part, 'tm')  22.2 us
    ppermute x3, waiting for transfers between devices, chip_pair(): far = lax.ppermute(strips, 'tile', [(j, j ^ 2) for j in range(count)])  21.8 us
    all_to_all x1, starting transfers between devices, body(): lax.all_to_all(stacked, 'tm', split_axis=2, concat_axis=0, tiled=True)  18.5 us
  transfers between devices with their start and end apart: 10, of which 4 were waited for; matrix products, arithmetic and copies ran while one was open for 66% of the time, Pallas kernels for 0%

profile of v4, /device:TPU:1, one launch (start us, length us, event | category | flops | bytes accessed | tf_op | source)
XLA Modules:
  0.0 569.8 jit_solution(7838343314106292220)
XLA Ops:
  8.8 2.6 collective-permute-start
  11.4 21.8 %collective-permute-done = f32[1024,256]{0,1:T(8,128)} collective-permute-done((f32[1024,256]{0,1:T(8,128)S(1)}, f32[1024,256]{0,1:T(8,128)}, u32[]{:S(2)}, u32[]{:S(2)}) %collective-permute-start) | collective-permute-done | bytes 1048608 | tf_op jit(solution)/shard_map/ppermute | solution.py:27
  36.2 2.4 collective-permute-start.1
  39.7 2.5 copy.111
  46.7 2.2 broadcast_select_fusion.4
  50.8 11.7 %cholesky.134 = f32[128,128]{1,0:T(8,128)S(1)} custom-call(f32[128,128]{1,0:T(8,128)S(1)} %fusion.76), custom_call_target="Cholesky" | custom-call | tf_op jit(solution)/shard_map/jit(cholesky)/cholesky | solution.py:54
  63.8 5.4 collective-permute-done.2
  70.9 9.8 %custom-call.12 = f32[1,128,128]{1,2,0:T(8,128)S(1)} custom-call(f32[1,128,128]{2,1,0:T(8,128)S(1)} %select_bitcast_fusion.7), custom_call_target="InvertDiagBlocksLowerTriangular" | custom-call | tf_op jit(solution)/shard_map/triangular_solve/custom-call.0 | solution.py:58
  81.9 4.7 fusion.1
  88.8 12.5 %cholesky.145 = f32[128,128]{1,0:T(8,128)S(1)} custom-call(f32[128,128]{1,0:T(8,128)} %fusion.74), custom_call_target="Cholesky" | custom-call | tf_op jit(solution)/shard_map/jit(cholesky)/cholesky | solution.py:54
  103.4 11.3 %custom-call.13 = f32[1,128,128]{1,2,0:T(8,128)} custom-call(f32[1,128,128]{2,1,0:T(8,128)} %fusion.53), custom_call_target="InvertDiagBlocksLowerTriangular" | custom-call | tf_op jit(solution)/shard_map/triangular_solve/custom-call.0 | solution.py:58
  117.0 2.0 slice_subtract_fusion.5
  121.5 11.7 %cholesky.156 = f32[128,128]{1,0:T(8,128)S(1)} custom-call(f32[128,128]{1,0:T(8,128)S(1)} %fusion.72), custom_call_target="Cholesky" | custom-call | tf_op jit(solution)/shard_map/jit(cholesky)/cholesky | solution.py:54
  134.6 9.8 %custom-call.14 = f32[1,128,128]{1,2,0:T(8,128)S(1)} custom-call(f32[1,128,128]{2,1,0:T(8,128)S(1)} %fusion.54), custom_call_target="InvertDiagBlocksLowerTriangular" | custom-call | tf_op jit(solution)/shard_map/triangular_solve/custom-call.0 | solution.py:58
  146.4 2.9 slice_subtract_fusion.6
  149.5 11.9 %cholesky.167 = f32[128,128]{1,0:T(8,128)S(1)} custom-call(f32[128,128]{1,0:T(8,128)S(1)} %fusion.70), custom_call_target="Cholesky" | custom-call | tf_op jit(solution)/shard_map/jit(cholesky)/cholesky | solution.py:54
  174.4 9.8 %custom-call.15 = f32[1,128,128]{1,2,0:T(8,128)S(1)} custom-call(f32[1,128,128]{2,1,0:T(8,128)S(1)} %select_bitcast_fusion.6), custom_call_target="InvertDiagBlocksLowerTriangular" | custom-call | tf_op jit(solution)/shard_map/triangular_solve/custom-call.0 | solution.py:58
  186.6 2.2 convolution_subtract_fusion.3
  193.5 13.2 %cholesky.178 = f32[128,128]{1,0:T(8,128)} custom-call(f32[128,128]{1,0:T(8,128)} %fusion.68), custom_call_target="Cholesky" | custom-call | tf_op jit(solution)/shard_map/jit(cholesky)/cholesky | solution.py:54
  208.2 2.1 fusion.55
  210.3 11.3 %custom-call.16 = f32[1,128,128]{1,2,0:T(8,128)} custom-call(f32[1,128,128]{2,1,0:T(8,128)} %fusion.55), custom_call_target="InvertDiagBlocksLowerTriangular" | custom-call | tf_op jit(solution)/shard_map/triangular_solve/custom-call.0 | solution.py:58
  231.7 13.5 %cholesky.189 = f32[128,128]{1,0:T(8,128)} custom-call(f32[128,128]{1,0:T(8,128)} %fusion.66), custom_call_target="Cholesky" | custom-call | tf_op jit(solution)/shard_map/jit(cholesky)/cholesky | solution.py:54
  246.8 2.1 fusion.56
  248.9 11.3 %custom-call.17 = f32[1,128,128]{1,2,0:T(8,128)} custom-call(f32[1,128,128]{2,1,0:T(8,128)} %fusion.56), custom_call_target="InvertDiagBlocksLowerTriangular" | custom-call | tf_op jit(solution)/shard_map/triangular_solve/custom-call.0 | solution.py:58
  269.6 13.2 %cholesky.200 = f32[128,128]{1,0:T(8,128)} custom-call(f32[128,128]{1,0:T(8,128)} %fusion.64), custom_call_target="Cholesky" | custom-call | tf_op jit(solution)/shard_map/jit(cholesky)/cholesky | solution.py:54
  284.3 2.1 fusion.57
  286.4 11.4 %custom-call.18 = f32[1,128,128]{1,2,0:T(8,128)} custom-call(f32[1,128,128]{2,1,0:T(8,128)} %fusion.57), custom_call_target="InvertDiagBlocksLowerTriangular" | custom-call | tf_op jit(solution)/shard_map/triangular_solve/custom-call.0 | solution.py:58
  306.2 13.2 %cholesky.211 = f32[128,128]{1,0:T(8,128)} custom-call(f32[128,128]{1,0:T(8,128)} %fusion.62), custom_call_target="Cholesky" | custom-call | tf_op jit(solution)/shard_map/jit(cholesky)/cholesky | solution.py:54
  324.5 2.1 fusion.58
  326.7 11.3 %custom-call.19 = f32[1,128,128]{1,2,0:T(8,128)} custom-call(f32[1,128,128]{2,1,0:T(8,128)} %fusion.58), custom_call_target="InvertDiagBlocksLowerTriangular" | custom-call | tf_op jit(solution)/shard_map/triangular_solve/custom-call.0 | solution.py:58
  350.8 4.2 broadcast_select_fusion
  356.4 2.6 copy.96
  359.0 2.2 broadcast_select_fusion.3
  368.5 2.5 copy.99
  371.0 2.6 fusion
  376.6 6.1 %slice_subtract_fusion = f32[896,2048]{1,0:T(8,128)S(1)} fusion(f32[1024,2048]{1,0:T(8,128)S(1)} %constant_dynamic-update-slice_fusion.7, f32[896,128]{1,0:T(8,128)S(1)} %copy-done.2, f32[128,2048]{1,0:T(8,128)S(1)} %get-tuple-element.71), kind=kOutput, calls=%fused_computation | convolution fusion | flops 2820407296 | bytes 16187392 | tf_op jit(solution)/shard_map/dot_general | solution.py:17
  383.7 5.5 slice_subtract_fusion.1
  390.3 4.5 slice_subtract_fusion.2
  395.8 3.6 slice_subtract_fusion.3
  400.5 2.9 slice_subtract_fusion.4
  412.9 3.4 collective-permute-start.7
  416.3 6.9 %fusion.2 = f32[1,1024,256]{2,1,0:T(8,128)S(1)} fusion(f32[1024,1024]{1,0:T(8,128)S(1)} %get-tuple-element.25, s32[]{:T(128)S(6)} %select_n.97, f32[1024,2048]{1,0:T(8,128)S(1)} %convolution_dynamic-update-slice_fusion), kind=kOutput, calls=%fused_computation.21 | convolution fusion | flops 3221487616 | bytes 6291460 | tf_op jit(solution)/shard_map/dot_general | solution.py:21
  423.2 7.1 %fusion.3 = f32[1,1024,256]{2,1,0:T(8,128)S(1)} fusion(f32[1024,1024]{1,0:T(8,128)S(1)} %get-tuple-element.25, s32[]{:T(128)S(6)} %select_n.97), kind=kOutput, calls=%fused_computation.23 | convolution fusion | flops 3221487616 | bytes 6291460 | tf_op jit(solution)/shard_map/dot_general | solution.py:21
  430.4 6.9 %fusion.4 = f32[1,1024,256]{2,1,0:T(8,128)S(1)} fusion(f32[1024,1024]{1,0:T(8,128)S(1)} %get-tuple-element.24, f32[2,1024,256]{2,1,0:T(8,128)S(1)} %copy-done.19, s32[]{:T(128)S(6)} %select_n.97), kind=kOutput, calls=%fused_computation.25 | convolution fusion | flops 3221487616 | bytes 7340036 | tf_op jit(solution)/shard_map/dot_general | solution.py:21
  437.5 22.2 %all-gather.3.cloned.1.call-done = f32[4096,64]{1,0:T(8,128)} async-done(((f32[64,64]{1,0:T(8,128)}), f32[4096,64]{1,0:T(8,128)}) %all-gather.3.cloned.1.call-update) | async-done | bytes 1048592 | tf_op jit(solution)/shard_map/all_gather | solution.py:94
  459.7 4.9 copy.100
  464.6 18.5 %all-to-all-start = ((f32[1,3,1024,256]{3,0,1,2:T(1,128)}), f32[1,3,1024,256]{3,0,1,2:T(1,128)S(1)}, u32[]{:S(2)}, u32[]{:S(2)}) async-start(f32[1,3,1024,256]{3,0,1,2:T(1,128)} %copy.100), calls=%async_computation | async-start | bytes 6291456 | tf_op jit(solution)/shard_map/all_to_all | solution.py:110
  488.1 71.8 %all-to-all-done = f32[1,3,1024,256]{3,0,1,2:T(1,128)S(1)} async-done(((f32[1,3,1024,256]{3,0,1,2:T(1,128)}), f32[1,3,1024,256]{3,0,1,2:T(1,128)S(1)}, u32[]{:S(2)}, u32[]{:S(2)}) %all-to-all-start) | async-done | bytes 3145760 | tf_op jit(solution)/shard_map/all_to_all | solution.py:110
  (219 shorter events, 131.7 us)
Async XLA Ops:
  7.2 452.6 %all-gather.3.cloned.1.call-start = ((), (), s32[]{:S(2)}) async-start(), calls=%async_computation.1 | async-start | bytes 2129920 | tf_op jit(solution)/shard_map/all_gather | solution.py:94
  8.8 24.4 %collective-permute-start = (f32[1024,256]{0,1:T(8,128)S(1)}, f32[1024,256]{0,1:T(8,128)}, u32[]{:S(2)}, u32[]{:S(2)}) collective-permute-start(f32[1024,256]{0,1:T(8,128)S(1)} %bitcast.224), channel_id=1, source_target_pairs={{0,2},{1,3},{2,0},{3,1},{4,6},{5,7},{6,4},{7,5},{8,10},{9,11},{10,... | collective-permute-start | bytes 3145736 | tf_op jit(solution)/shard_map/ppermute | solution.py:27
  11.4 27.2 %copy-start.20 = (f32[2,1024,256]{2,1,0:T(8,128)S(1)}, f32[2,1024,256]{2,1,0:T(8,128)}, u32[]{:S(2)}) copy-start(f32[2,1024,256]{2,1,0:T(8,128)} %param.8) | copy-start | bytes 6291460
  36.2 10.5 %collective-permute-start.1 = (f32[2,1024,256]{1,2,0:T(8,128)}, f32[2,1024,256]{1,2,0:T(8,128)}, u32[]{:S(2)}, u32[]{:S(2)}) collective-permute-start(f32[2,1024,256]{1,2,0:T(8,128)} %pad_maximum_fusion.3), channel_id=1, source_target_pairs={{0,1},{1,0},{2,3},{3,2},{4,5},{5,4},{6,7},{7,6},{8,9},{9,8},{10,11... | collective-permute-start | bytes 6291464 | tf_op jit(solution)/shard_map/ppermute | solution.py:37
  42.2 27.0 %collective-permute-start.2 = (f32[1024,256]{0,1:T(8,128)}, f32[1024,256]{0,1:T(8,128)}, u32[]{:S(2)}, u32[]{:S(2)}) collective-permute-start(f32[1024,256]{0,1:T(8,128)} %bitcast.226), channel_id=1, source_target_pairs={{4,0},{8,4},{12,8},{16,12},{20,16},{24,20},{28,24},{32,28},{36,32}... | collective-permute-start | bytes 3145736 | tf_op jit(solution)/shard_map/ppermute | solution.py:13
  50.6 31.3 %copy-start.7 = (f32[1024,256]{0,1:T(8,128)}, f32[1024,256]{0,1:T(8,128)S(1)}, u32[]{:S(2)}) copy-start(f32[1024,256]{0,1:T(8,128)S(1)} %get-tuple-element.49) | copy-start | bytes 3145732
  69.2 98.5 %collective-permute-start.4 = (f32[1024,256]{0,1:T(8,128)}, f32[1024,256]{0,1:T(8,128)}, u32[]{:S(2)}, u32[]{:S(2)}) collective-permute-start(f32[1024,256]{0,1:T(8,128)} %collective-permute-done.2), channel_id=1, source_target_pairs={{0,2},{1,3},{2,0},{3,1},{4,6},{5,7},{6,4},{7,5},{8,10},{9,11},{10,... | collective-permute-start | bytes 3145736 | tf_op jit(solution)/shard_map/ppermute | solution.py:27
  70.6 100.2 %collective-permute-start.3 = (f32[1024,256]{0,1:T(8,128)}, f32[1024,256]{0,1:T(8,128)}, u32[]{:S(2)}, u32[]{:S(2)}) collective-permute-start(f32[1024,256]{0,1:T(8,128)} %bitcast.5), channel_id=1, source_target_pairs={{0,2},{1,3},{2,0},{3,1},{4,6},{5,7},{6,4},{7,5},{8,10},{9,11},{10,... | collective-permute-start | bytes 3145736 | tf_op jit(solution)/shard_map/ppermute | solution.py:27
  81.0 0.9 copy-start.36
  81.9 4.7 copy-start.1
  116.2 46.7 %copy-start.32 = (f32[128,128]{1,0:T(8,128)}, f32[128,128]{1,0:T(8,128)S(1)}, u32[]{:S(2)}) copy-start(f32[128,128]{1,0:T(8,128)S(1)} %fusion.45) | copy-start | bytes 196612
  117.0 2.1 copy-start.3
  119.1 1.4 copy-start.5
  120.5 40.9 %copy-start.37 = (f32[128,128]{1,0:T(8,128)S(1)}, f32[128,128]{1,0:T(8,128)}, u32[]{:S(2)}) copy-start(f32[128,128]{1,0:T(8,128)} %copy-done.36) | copy-start | bytes 196612
  120.5 41.7 %copy-start.2 = (f32[896,128]{1,0:T(8,128)S(1)}, f32[896,128]{1,0:T(8,128)}, u32[]{:S(2)}) copy-start(f32[896,128]{1,0:T(8,128)} %copy-done.1) | copy-start | bytes 1376260
  144.7 21.0 %copy-start.34 = (f32[128,128]{1,0:T(8,128)}, f32[128,128]{1,0:T(8,128)S(1)}, u32[]{:S(2)}) copy-start(f32[128,128]{1,0:T(8,128)S(1)} %fusion.43) | copy-start | bytes 196612
  144.7 19.7 %copy-start.4 = (f32[768,128]{1,0:T(8,128)S(1)}, f32[768,128]{1,0:T(8,128)}, u32[]{:S(2)}) copy-start(f32[768,128]{1,0:T(8,128)} %copy-done.3) | copy-start | bytes 1179652
  149.3 20.1 %copy-start.8 = (f32[640,640]{0,1:T(8,128)}, f32[640,640]{0,1:T(8,128)S(1)}, u32[]{:S(2)}) copy-start(f32[640,640]{0,1:T(8,128)S(1)} %slice_subtract_fusion.6) | copy-start | bytes 4915204
  172.8 177.9 %collective-permute-start.6 = (f32[2,1024,256]{1,2,0:T(8,128)}, f32[2,1024,256]{1,2,0:T(8,128)}, u32[]{:S(2)}, u32[]{:S(2)}) collective-permute-start(f32[2,1024,256]{1,2,0:T(8,128)} %pad_maximum_fusion.5), channel_id=1, source_target_pairs={{0,1},{1,0},{2,3},{3,2},{4,5},{5,4},{6,7},{7,6},{8,9},{9,8},{10,11... | collective-permute-start | bytes 6291464 | tf_op jit(solution)/shard_map/ppermute | solution.py:37
  174.2 184.8 %collective-permute-start.5 = (f32[2,1024,256]{1,2,0:T(8,128)S(1)}, f32[2,1024,256]{1,2,0:T(8,128)}, u32[]{:S(2)}, u32[]{:S(2)}) collective-permute-start(f32[2,1024,256]{1,2,0:T(8,128)S(1)} %pad_maximum_fusion.4), channel_id=1, source_target_pairs={{0,1},{1,0},{2,3},{3,2},{4,5},{5,4},{6,7},{7,6},{8,9},{9,8},{10,11... | collective-permute-start | bytes 6291464 | tf_op jit(solution)/shard_map/ppermute | solution.py:37
  188.9 1.0 copy-start.15
  224.8 0.7 copy-start.9
  227.2 0.8 copy-start.18
  261.3 0.6 copy-start.28
  263.2 0.6 copy-start.16
  265.2 0.7 copy-start.23
  343.9 4.0 copy-start.39
  361.2 3.0 copy-start.6
  364.2 3.0 copy-start.14
  371.0 2.6 copy-start.11
  373.6 1.2 copy-start.12
  373.6 1.5 copy-start.13
  373.8 1.7 copy-start.38
  376.5 6.1 %copy-start.33 = (f32[128,128]{1,0:T(8,128)S(1)}, f32[128,128]{1,0:T(8,128)}, u32[]{:S(2)}) copy-start(f32[128,128]{1,0:T(8,128)} %copy-done.32) | copy-start | bytes 196612
  383.7 5.5 copy-start.35
  390.3 4.5 copy-start.25
  395.8 3.6 copy-start.27
  399.4 1.0 copy-start.10
  400.5 3.0 copy-start.29
  403.4 1.1 copy-start.17
  404.4 1.9 copy-start.31
  404.5 2.9 copy-start.22
  406.3 2.1 copy-start.40
  411.1 19.3 %copy-start = (f32[1024,1024]{1,0:T(8,128)}, f32[1024,1024]{1,0:T(8,128)S(1)}, u32[]{:S(2)}) copy-start(f32[1024,1024]{1,0:T(8,128)S(1)} %get-tuple-element.24) | copy-start | bytes 12582916
  412.9 46.8 %collective-permute-start.7 = (f32[64,256]{1,0:T(8,128)S(1)}, f32[64,256]{1,0:T(8,128)S(1)}, u32[]{:S(2)}, u32[]{:S(2)}) collective-permute-start(f32[64,256]{1,0:T(8,128)S(1)} %convolution_negate_fusion.2), channel_id=1, source_target_pairs={{0,4},{4,8},{8,12},{12,16},{16,20},{20,24},{24,28},{28,32},{32,36}... | collective-permute-start | bytes 196616 | tf_op jit(solution)/shard_map/ppermute | solution.py:13
  423.2 7.2 %copy-start.19 = (f32[2,1024,256]{2,1,0:T(8,128)S(1)}, f32[2,1024,256]{2,1,0:T(8,128)}, u32[]{:S(2)}) copy-start(f32[2,1024,256]{2,1,0:T(8,128)} %param.7) | copy-start | bytes 6291460
  464.6 95.2 %all-to-all-start = ((f32[1,3,1024,256]{3,0,1,2:T(1,128)}), f32[1,3,1024,256]{3,0,1,2:T(1,128)S(1)}, u32[]{:S(2)}, u32[]{:S(2)}) async-start(f32[1,3,1024,256]{3,0,1,2:T(1,128)} %copy.100), calls=%async_computation | async-start | bytes 6291456 | tf_op jit(solution)/shard_map/all_to_all | solution.py:110
  483.1 3.7 copy-start.41
  (4 other events, 2.5 us)
Sparse Core Ops, SparseCore 0:
  350.9 108.8 all-gather.2
